TPU v7x, 128 devices: a whole 4x4x4 slice. The times are simulated.
128 devices in a mesh: dp: 4 (over z), expert: 32 (over x, y, core).
Axes of the slice: x: 4, y: 4, z: 4, core: 2. Of those that a mesh axis runs over, the one named last changes fastest.
Arguments:
- tokens: bfloat16 [20480, 2048], P(('dp', 'expert')), may hold values from -6 to 6
- target: bfloat16 [20480, 2048], P(('dp', 'expert')), may hold values from -6 to 6
- expert_ids: int32 [20480, 4], P(('dp', 'expert')), may hold values from 0 to 63, all different within a row; in each aligned block of 160 rows (0 to 159, 160 to 319, ...) at most 15 rows name the same one
- gates: float32 [20480, 4], P(('dp', 'expert')), may hold values from 0.05 to 0.5
- w_in: bfloat16 [2048, 64, 1536], P(None, 'expert'), may hold values from -0.125 to 0.125
- w_out: bfloat16 [768, 64, 2048], P(None, 'expert'), may hold values from -0.21875 to 0.21875
Outputs:
- grad_tokens: bfloat16 [20480, 2048], P(('dp', 'expert'))
- grad_in: bfloat16 [2048, 64, 1536], P('dp', 'expert')
- grad_out: bfloat16 [768, 64, 2048], P(None, 'expert', 'dp')
Inputs may be any that keep to these rules, and one draw needn't show every extreme that they name: `expert_ids`: each token names 4 different experts; in each aligned block of 160 rows (the tokens of one device) no expert is named by more than 15 rows, a bound that some block reaches.
All inputs are finite; a program needn't handle non-finite values.
Results may differ from a plain program's by a relative error of at most 0.012.
Values may be sent and summed in bfloat16 or wider, within the bound.
No kernel may reach another device: no remote copies, remote signals or barrier semaphores. Data moves between devices by JAX's collectives and lax.ppermute only.
A program may use at most 192 MiB of HBM per device.

v0:
```python
import jax
import jax.numpy as jnp
from jax import lax
from jax.sharding import PartitionSpec as P


def swiglu_forward(preact, hidden):
    gate_part = preact[..., :hidden]
    up_part = preact[..., hidden:]
    return gate_part * jax.nn.sigmoid(gate_part) * up_part


def swiglu_backward(preact, upstream, hidden):
    gate_part = preact[..., :hidden]
    up_part = preact[..., hidden:]
    sigmoid_value = jax.nn.sigmoid(gate_part)
    silu_value = gate_part * sigmoid_value
    derivative = sigmoid_value * (1.0 + gate_part * (1.0 - sigmoid_value))
    return jnp.concatenate([upstream * up_part * derivative, upstream * silu_value], axis=-1)


def per_device(tokens, target, expert_ids, gates, w_in, w_out):
    tok_rows, model_width = tokens.shape
    route_count = expert_ids.shape[1]
    hidden = w_out.shape[0]
    local_experts = w_in.shape[1]
    expert_peers = lax.axis_size("expert")
    experts_all = local_experts * expert_peers
    capacity = 3 * tok_rows * route_count // (2 * experts_all)
    routes = tok_rows * route_count
    flat_ids = expert_ids.reshape(routes)
    matches = (flat_ids[:, None] == jnp.arange(experts_all, dtype=jnp.int32)[None, :]).astype(
        jnp.int32
    )
    ranking = jnp.sum((jnp.cumsum(matches, axis=0) - 1) * matches, axis=1)
    slot_index = flat_ids * capacity + ranking
    weights_flat = gates.reshape(routes, 1)

    def dispatch(route_rows):
        buffer = (
            jnp.zeros((experts_all * capacity, model_width), route_rows.dtype)
            .at[slot_index]
            .set(route_rows)
        )
        return buffer.reshape(expert_peers, local_experts, capacity, model_width)

    sent_rows = lax.all_to_all(
        dispatch(jnp.repeat(tokens, route_count, axis=0)),
        "expert",
        split_axis=0,
        concat_axis=0,
        tiled=True,
    )
    preact = jnp.einsum("sekd,deh->sekh", sent_rows, w_in, preferred_element_type=jnp.float32)
    activation = swiglu_forward(preact, hidden).astype(jnp.bfloat16)
    outputs = jnp.einsum(
        "sekh,hed->sekd", activation, w_out, preferred_element_type=jnp.float32
    ).astype(jnp.bfloat16)
    returned = lax.all_to_all(outputs, "expert", split_axis=0, concat_axis=0, tiled=True)
    route_rows = returned.reshape(experts_all * capacity, model_width)[slot_index]
    student = tokens.astype(jnp.float32) + jnp.sum(
        route_rows.astype(jnp.float32).reshape(tok_rows, route_count, model_width)
        * weights_flat.reshape(tok_rows, route_count, 1),
        axis=1,
    )
    residual_grad = student - target.astype(jnp.float32)
    scaled = (weights_flat * jnp.repeat(residual_grad, route_count, axis=0)).astype(jnp.bfloat16)
    sent_grads = lax.all_to_all(dispatch(scaled), "expert", split_axis=0, concat_axis=0, tiled=True)
    act_grad = jnp.einsum("sekd,hed->sekh", sent_grads, w_out, preferred_element_type=jnp.float32)
    pre_grad = swiglu_backward(preact, act_grad, hidden).astype(jnp.bfloat16)
    input_grads = jnp.einsum(
        "sekh,deh->sekd", pre_grad, w_in, preferred_element_type=jnp.float32
    ).astype(jnp.bfloat16)
    returned_grads = lax.all_to_all(input_grads, "expert", split_axis=0, concat_axis=0, tiled=True)
    route_back = returned_grads.reshape(experts_all * capacity, model_width)[slot_index]
    grad_tokens = (
        residual_grad
        + jnp.sum(
            route_back.astype(jnp.float32).reshape(tok_rows, route_count, model_width), axis=1
        )
    ).astype(jnp.bfloat16)
    term_in = jnp.einsum("sekd,sekh->deh", sent_rows, pre_grad, preferred_element_type=jnp.float32)
    term_out = jnp.einsum(
        "sekh,sekd->hed", activation, sent_grads, preferred_element_type=jnp.float32
    )
    grad_in, grad_out = (
        lax.psum_scatter(
            term_in.astype(jnp.bfloat16), "dp", scatter_dimension=0, tiled=True
        ).astype(jnp.float32),
        lax.psum_scatter(
            term_out.astype(jnp.bfloat16), "dp", scatter_dimension=2, tiled=True
        ).astype(jnp.float32),
    )
    return (grad_tokens, grad_in.astype(jnp.bfloat16), grad_out.astype(jnp.bfloat16))


def solution(mesh):
    in_specs = (
        P(("dp", "expert"), None),
        P(("dp", "expert"), None),
        P(("dp", "expert"), None),
        P(("dp", "expert"), None),
        P(None, "expert", None),
        P(None, "expert", None),
    )
    out_specs = (P(("dp", "expert"), None), P("dp", "expert", None), P(None, "expert", "dp"))
    return jax.shard_map(
        per_device, mesh=mesh, in_specs=in_specs, out_specs=out_specs, check_vma=False
    )
```

profile of v0, /device:TPU:1, one launch (start us, length us, event | category | flops | bytes accessed | tf_op | source)
XLA Modules:
  0.0 512.2 jit_solution(18288562466569278043)
XLA Ops:
  7.2 0.7 broadcast_multiply_fusion
  7.9 0.8 copy.51
  9.1 1.5 reduce-window.6
  10.6 0.3 slice_reduce_fusion
  10.9 2.4 broadcast_in_dim.4
  13.3 2.8 reshape.112
  16.2 10.3 %scatter_custom_fusion = bf16[960,2048]{1,0:T(8,128)(2,1)} fusion(s32[640]{0:T(1024)S(1)} %fusion.33, bf16[640,2048]{1,0:T(8,128)(2,1)} %reshape.112, bf16[]{:T(256)} %constant.7.clone.1), kind=kCustom, calls=%fused_computation.37 | custom fusion | bytes 3932672 | tf_op jit(solution)/shard_map/scatter | solution.py:43
  26.5 5.1 reshape.85
  31.6 6.5 %copy.54 = bf16[32,2,15,2048]{3,1,2,0:T(2,128)(2,1)S(1)} copy(bf16[32,2,15,2048]{3,2,1,0:T(8,128)(2,1)} %reshape.85) | data formatting | bytes 7864320 | tf_op jit(solution)/shard_map/reshape | solution.py:45
  38.1 56.3 %all_to_all.20 = bf16[32,2,15,2048]{3,1,2,0:T(2,128)(2,1)S(1)} all-to-all(bf16[32,2,15,2048]{3,1,2,0:T(2,128)(2,1)S(1)} %copy.54), channel_id=1, replica_groups=mesh['dp'=4,'expert'=32] {'expert'}, dimensions={0} | all-to-all | bytes 7864320 | tf_op jit(solution)/shard_map/all_to_all | solution.py:47
  94.4 13.4 %fusion.10 = f32[32,2,15,1536]{3,0,2,1:T(8,128)S(1)} fusion(bf16[2048,2,1536,1]{2,1,0,3:T(2,128)(2,1)} %bitcast.54, bf16[32,2,15,2048]{3,1,2,0:T(2,128)(2,1)S(1)} %all_to_all.20), kind=kOutput, calls=%fused_computation.18 | convolution fusion | flops 6039797760 | bytes 22413312 | tf_op jit(solution)/shard_map/sekd,deh->sekh/dot_general | solution.py:54
  107.9 2.5 copy-done
  110.4 0.9 multiply_convert_fusion.1
  111.3 1.1 copy-done.5
  112.4 11.4 %convert_bitcast_fusion.1 = bf16[32,2,15,2048]{3,0,2,1:T(8,128)(2,1)S(1)} fusion(bf16[32,2,15,768]{3,0,2,1:T(8,128)(2,1)S(1)} %multiply_convert_fusion.1, bf16[768,2,2048,1]{2,1,0,3:T(2,128)(2,1)} %bitcast.56), kind=kOutput, calls=%fused_computation.20 | convolution fusion | flops 3021864960 | bytes 11698176 | tf_op jit(solution)/shard_map/sekh,hed->sekd/dot_general | solution.py:56
  123.8 6.0 %copy.58 = bf16[32,2,15,2048]{3,1,2,0:T(2,128)(2,1)} copy(bf16[32,2,15,2048]{3,0,2,1:T(8,128)(2,1)S(1)} %convert_bitcast_fusion.1) | data formatting | bytes 7864320 | tf_op jit(solution)/shard_map/convert_element_type | solution.py:58
  129.8 4.8 all-to-all-start.1
  134.8 48.6 %all-to-all-done.1 = bf16[32,2,15,2048]{3,1,2,0:T(2,128)(2,1)} async-done(((bf16[32,2,15,2048]{3,1,2,0:T(2,128)(2,1)}), bf16[32,2,15,2048]{3,1,2,0:T(2,128)(2,1)}, u32[]{:S(2)}, u32[]{:S(2)}) %all-to-all-start.1) | async-done | bytes 3932192 | tf_op jit(solution)/shard_map/all_to_all | solution.py:59
  183.4 5.9 %copy.59 = bf16[32,2,15,2048]{3,2,1,0:T(8,128)(2,1)} copy(bf16[32,2,15,2048]{3,1,2,0:T(2,128)(2,1)} %all-to-all-done.1) | data formatting | bytes 7864320 | tf_op jit(solution)/shard_map/all_to_all | solution.py:59
  189.3 5.6 %reshape.86 = bf16[960,2048]{1,0:T(8,128)(2,1)} reshape(bf16[32,2,15,2048]{3,2,1,0:T(8,128)(2,1)} %copy.59) | data formatting | bytes 7864320 | tf_op jit(solution)/shard_map/reshape | solution.py:60
  194.9 9.0 %gather_fusion = bf16[640,2048]{1,0:T(8,128)(2,1)S(1)} fusion(bf16[960,2048]{1,0:T(8,128)(2,1)} %reshape.86, s32[1024]{0:T(1024)S(1)} %pad_clamp_fusion), kind=kCustom, calls=%fused_computation | custom fusion | bytes 5245440 | tf_op jit(solution)/shard_map/gather | solution.py:60
  203.9 4.1 reshape.90
  207.9 6.7 %multiply_reduce_fusion = f32[160,2048]{1,0:T(8,128)S(1)} fusion(f32[160,4,2048]{2,1,0:T(4,128)} %reshape.90, f32[160,4]{1,0:T(8,128)S(1)} %copy.60), kind=kLoop, calls=%fused_computation.17 | loop fusion | flops 2293760 | bytes 6556160 | tf_op jit(solution)/shard_map/reduce_sum | solution.py:61
  214.7 0.3 convert_subtract_fusion
  214.9 3.8 broadcast_in_dim.5
  218.7 7.3 %reshape.87 = f32[640,2048]{1,0:T(8,128)} reshape(f32[160,4,2048]{2,1,0:T(4,128)} %broadcast_in_dim.5) | data formatting | bytes 10485760 | tf_op jit(solution)/shard_map/reshape | solution.py:67
  226.0 14.6 %scatter_custom_fusion.1 = bf16[960,2048]{1,0:T(8,128)(2,1)} fusion(s32[640]{0:T(1024)S(1)} %fusion.33, f32[640,2048]{1,0:T(8,128)} %reshape.87, f32[640]{0:T(1024)S(1)} %mul.67, bf16[]{:T(256)} %constant.7.clone.1), kind=kCustom, calls=%fused_computation.34 | custom fusion | flops 2621440 | bytes 9179138 | tf_op jit(solution)/shard_map/scatter | solution.py:43
  240.6 5.1 %reshape.88 = bf16[32,2,15,2048]{3,2,1,0:T(8,128)(2,1)} reshape(bf16[960,2048]{1,0:T(8,128)(2,1)} %scatter_custom_fusion.1) | data formatting | bytes 7864320 | tf_op jit(solution)/shard_map/reshape | solution.py:45
  245.8 6.5 %copy.62 = bf16[32,2,15,2048]{3,1,2,0:T(2,128)(2,1)S(1)} copy(bf16[32,2,15,2048]{3,2,1,0:T(8,128)(2,1)} %reshape.88) | data formatting | bytes 7864320 | tf_op jit(solution)/shard_map/reshape | solution.py:45
  252.2 55.1 %all_to_all.21 = bf16[32,2,15,2048]{3,1,2,0:T(2,128)(2,1)S(1)} all-to-all(bf16[32,2,15,2048]{3,1,2,0:T(2,128)(2,1)S(1)} %copy.62), channel_id=1, replica_groups=mesh['dp'=4,'expert'=32] {'expert'}, dimensions={0} | all-to-all | bytes 7864320 | tf_op jit(solution)/shard_map/all_to_all | solution.py:68
  307.3 1.9 copy-done.3
  309.2 7.6 %fusion.5 = bf16[768,2,2048]{0,2,1:T(8,128)(2,1)} fusion(bf16[32,2,15,768]{3,0,2,1:T(8,128)(2,1)S(1)} %copy-done.6, bf16[32,2,15,2048]{3,1,2,0:T(2,128)(2,1)S(1)} %all_to_all.21), kind=kOutput, calls=%fused_computation.11 | convolution fusion | flops 3023044608 | bytes 11698176 | tf_op jit(solution)/shard_map/sekh,sekd->hed/dot_general | solution.py:83
  316.9 12.9 %fusion.22 = (bf16[32,2,15,768]{3,0,2,1:T(8,128)(2,1)S(1)}, bf16[32,2,15,768]{3,0,2,1:T(8,128)(2,1)S(1)}) fusion(f32[32,2,15,1536]{3,0,2,1:T(8,128)} %copy-done, bf16[768,2,2048,1]{2,1,0,3:T(2,128)(2,1)} %bitcast.57, bf16[32,2,15,2048]{3,1,2,0:T(2,128)(2,1)} %copy-done.3), kind=kOutput, calls=%fused_computation.29 | convolution fusion | flops 3029483520 | bytes 19070976 | tf_op jit(solution)/shard_map/sekd,hed->sekh/dot_general | solution.py:69
  329.8 1.1 copy-done.9
  330.9 0.5 copy-done.10
  331.4 11.0 %fusion.4 = bf16[2048,2,1536]{0,2,1:T(8,128)(2,1)} fusion(bf16[32,2,15,2048]{3,1,2,0:T(2,128)(2,1)S(1)} %copy-done.2, bf16[32,2,15,768]{3,0,2,1:T(8,128)(2,1)S(1)} %get-tuple-element.16, bf16[32,2,15,768]{3,0,2,1:T(8,128)(2,1)S(1)} %get-tuple-element.15), kind=kOutput, calls=%fused_computation.10 | convolution fusion | flops 6051987456 | bytes 19464192 | tf_op jit(solution)/shard_map/sekd,sekh->deh/dot_general | solution.py:82
  342.4 13.4 %convert_bitcast_fusion = bf16[32,2,15,2048]{3,0,2,1:T(8,128)(2,1)} fusion(bf16[2048,2,1536,1]{2,1,0,3:T(2,128)(2,1)} %bitcast.55, bf16[32,2,15,768]{3,0,2,1:T(8,128)(2,1)} %copy-done.10, bf16[32,2,15,768]{3,0,2,1:T(8,128)(2,1)} %copy-done.9), kind=kOutput, calls=%fused_computation.19 | convolution fusion | flops 6047662080 | bytes 19464192 | tf_op jit(solution)/shard_map/sekh,deh->sekd/dot_general | solution.py:71
  355.8 6.2 %copy.66 = bf16[32,2,15,2048]{3,1,2,0:T(2,128)(2,1)S(1)} copy(bf16[32,2,15,2048]{3,0,2,1:T(8,128)(2,1)} %convert_bitcast_fusion) | data formatting | bytes 7864320 | tf_op jit(solution)/shard_map/convert_element_type | solution.py:73
  362.0 51.6 %all_to_all.22 = bf16[32,2,15,2048]{3,1,2,0:T(2,128)(2,1)S(1)} all-to-all(bf16[32,2,15,2048]{3,1,2,0:T(2,128)(2,1)S(1)} %copy.66), channel_id=1, replica_groups=mesh['dp'=4,'expert'=32] {'expert'}, dimensions={0} | all-to-all | bytes 7864320 | tf_op jit(solution)/shard_map/all_to_all | solution.py:74
  413.6 3.8 copy.67
  417.4 5.2 %reshape.89 = bf16[960,2048]{1,0:T(8,128)(2,1)} reshape(bf16[32,2,15,2048]{3,2,1,0:T(8,128)(2,1)} %copy.67) | data formatting | bytes 7864320 | tf_op jit(solution)/shard_map/reshape | solution.py:75
  422.6 9.5 %gather_fusion.1 = bf16[640,2048]{1,0:T(8,128)(2,1)} fusion(bf16[960,2048]{1,0:T(8,128)(2,1)} %reshape.89, s32[1024]{0:T(1024)S(1)} %pad_clamp_fusion), kind=kCustom, calls=%fused_computation.1 | custom fusion | bytes 5245440 | tf_op jit(solution)/shard_map/gather | solution.py:75
  432.1 6.0 %reshape.91 = f32[160,4,2048]{2,1,0:T(4,128)} reshape(bf16[640,2048]{1,0:T(8,128)(2,1)} %gather_fusion.1) | data formatting | bytes 7864320 | tf_op jit(solution)/shard_map/convert_element_type | solution.py:79
  438.1 5.8 %reduce_sum.32 = f32[160,2048]{1,0:T(8,128)S(1)} reduce(f32[160,4,2048]{2,1,0:T(4,128)} %reshape.91, f32[]{:T(128)} %constant.19.clone.1), dimensions={1}, to_apply=%region_6.7 | reduce | flops 983040 | bytes 6553604 | tf_op jit(solution)/shard_map/reduce_sum | solution.py:78
  444.0 1.0 add_convert_fusion
  444.9 5.0 copy.71
  449.9 46.5 %reduce-scatter.3.cloned.1.call-done = bf16[512,2,1536]{0,2,1:T(8,128)(2,1)} async-done(((bf16[2048,2,1536]{0,2,1:T(8,128)(2,1)}), bf16[512,2,1536]{0,2,1:T(8,128)(2,1)}) %reduce-scatter.3.cloned.1.call-update) | async-done | bytes 3145744 | tf_op jit(solution)/shard_map/reduce_scatter | solution.py:87
  496.4 8.7 %copy.70 = bf16[512,2,1536]{2,1,0:T(2,128)(2,1)} copy(bf16[512,2,1536]{0,2,1:T(8,128)(2,1)} %reduce-scatter.3.cloned.1.call-done) | data formatting | bytes 6291456
  (33 shorter events, 1.0 us)
Async XLA Ops:
  94.4 13.4 %copy-start.1 = (bf16[32,2,15,2048]{3,1,2,0:T(2,128)(2,1)}, bf16[32,2,15,2048]{3,1,2,0:T(2,128)(2,1)S(1)}, u32[]{:S(2)}) copy-start(bf16[32,2,15,2048]{3,1,2,0:T(2,128)(2,1)S(1)} %all_to_all.20) | copy-start | bytes 11796484
  107.9 2.5 copy-start
  111.3 1.1 copy-start.5
  129.8 4.8 copy-start.8
  129.8 53.6 %all-to-all-start.1 = ((bf16[32,2,15,2048]{3,1,2,0:T(2,128)(2,1)}), bf16[32,2,15,2048]{3,1,2,0:T(2,128)(2,1)}, u32[]{:S(2)}, u32[]{:S(2)}) async-start(bf16[32,2,15,2048]{3,1,2,0:T(2,128)(2,1)} %copy.58), calls=%async_computation.1 | async-start | bytes 7864320 | tf_op jit(solution)/shard_map/all_to_all | solution.py:59
  134.5 310.4 %reduce-scatter.5.cloned.1.call-start = ((), (), s32[]{:S(2)}) async-start(), calls=%async_computation.7 | async-start | bytes 7864320 | tf_op jit(solution)/shard_map/reduce_scatter | solution.py:90
  207.9 6.7 %copy-start.4 = (bf16[160,2048]{1,0:T(8,128)(2,1)S(1)}, bf16[160,2048]{1,0:T(8,128)(2,1)}, u32[]{:S(2)}) copy-start(bf16[160,2048]{1,0:T(8,128)(2,1)} %param.6) | copy-start | bytes 1966084
  207.9 6.7 %copy-start.7 = (bf16[160,2048]{1,0:T(8,128)(2,1)S(1)}, bf16[160,2048]{1,0:T(8,128)(2,1)}, u32[]{:S(2)}) copy-start(bf16[160,2048]{1,0:T(8,128)(2,1)} %param.7) | copy-start | bytes 1966084
  252.2 57.0 %copy-start.6 = (bf16[32,2,15,768]{3,0,2,1:T(8,128)(2,1)S(1)}, bf16[32,2,15,768]{3,0,2,1:T(8,128)(2,1)}, u32[]{:S(2)}) copy-start(bf16[32,2,15,768]{3,0,2,1:T(8,128)(2,1)} %copy-done.5) | copy-start | bytes 4423684
  307.3 1.9 copy-start.3
  316.8 179.6 %reduce-scatter.3.cloned.1.call-start = ((), (), s32[]{:S(2)}) async-start(), calls=%async_computation.6 | async-start | bytes 15728640 | tf_op jit(solution)/shard_map/reduce_scatter | solution.py:87
  316.9 14.5 %copy-start.2 = (bf16[32,2,15,2048]{3,1,2,0:T(2,128)(2,1)S(1)}, bf16[32,2,15,2048]{3,1,2,0:T(2,128)(2,1)}, u32[]{:S(2)}) copy-start(bf16[32,2,15,2048]{3,1,2,0:T(2,128)(2,1)} %copy-done.1) | copy-start | bytes 11796484
  329.8 1.1 copy-start.9
  329.8 1.6 copy-start.10
Sparse Core Ops, SparseCore 0:
  317.0 62.6 reduce-scatter.4
  382.1 114.2 reduce-scatter.2
where the time goes:
time: 522 us; the launch traced here: 512 us
  blocking collectives  163 us (31%)
  local copies, waits for them, and re-layouts  133 us (25%)
  waiting for transfers between devices  95.1 us (18%)
  matrix products  69.7 us (13%)
  other arithmetic  31.7 us (6%)
  between operations  14.5 us (3%)
    all_to_all x1, blocking collectives, per_device(): lax.all_to_all(dispatch(jnp.repeat(tokens, route_count, axis=0)), 'expert...  56.3 us
    all_to_all x1, blocking collectives, per_device(): lax.all_to_all(dispatch(scaled), 'expert', split_axis=0, concat_axis=0, t...  55.1 us
    all_to_all x1, blocking collectives, per_device(): lax.all_to_all(input_grads, 'expert', split_axis=0, concat_axis=0, tiled=...  51.6 us
    all_to_all x1, waiting for transfers between devices, per_device(): lax.all_to_all(outputs, 'expert', split_axis=0, concat_axis=0, tiled=True)  48.6 us
    reduce_scatter x1, waiting for transfers between devices, per_device(): lax.psum_scatter(term_in.astype(jnp.bfloat16), 'dp', scatter_dimension=0,...  46.5 us
    reshape x4, local copies, waits for them, and re-layouts, dispatch(): return buffer.reshape(expert_peers, local_experts, capacity, model_width)  23.2 us
    unnamed x26, local copies, waits for them, and re-layouts  21.8 us
    scatter x1, other arithmetic, dispatch(): buffer = jnp.zeros((experts_all * capacity, model_width), route_rows.dtyp...  14.6 us
  transfers between devices with their start and end apart: 3, of which 2 were waited for; matrix products, arithmetic and copies ran while one was open for 16% of the time, Pallas kernels for 0%

commit v1 on v0

--- a/solution.py
+++ b/solution.py
@@ -27,57 +27,54 @@
     expert_peers = lax.axis_size("expert")
     experts_all = local_experts * expert_peers
     capacity = 3 * tok_rows * route_count // (2 * experts_all)
+    slots_per = -(-capacity // 16) * 16
+    slot_total = experts_all * slots_per
     routes = tok_rows * route_count
     flat_ids = expert_ids.reshape(routes)
     matches = (flat_ids[:, None] == jnp.arange(experts_all, dtype=jnp.int32)[None, :]).astype(
         jnp.int32
     )
     ranking = jnp.sum((jnp.cumsum(matches, axis=0) - 1) * matches, axis=1)
-    slot_index = flat_ids * capacity + ranking
-    weights_flat = gates.reshape(routes, 1)
+    slot_index = flat_ids * slots_per + ranking
+    route_onehot = (slot_index[:, None] == jnp.arange(slot_total, dtype=jnp.int32)[None, :]).astype(
+        jnp.bfloat16
+    )
+    token_onehot = jnp.sum(
+        route_onehot.reshape(tok_rows, route_count, slot_total).astype(jnp.float32), axis=1
+    ).astype(jnp.bfloat16)
+    gate_rows = gates.reshape(tok_rows, route_count)
 
-    def dispatch(route_rows):
-        buffer = (
-            jnp.zeros((experts_all * capacity, model_width), route_rows.dtype)
-            .at[slot_index]
-            .set(route_rows)
-        )
-        return buffer.reshape(expert_peers, local_experts, capacity, model_width)
+    def to_slots(onehot, rows):
+        buffer = lax.dot_general(
+            onehot, rows, (((0,), (0,)), ((), ())), preferred_element_type=jnp.float32
+        ).astype(jnp.bfloat16)
+        return buffer.reshape(expert_peers, local_experts, slots_per, model_width)
 
-    sent_rows = lax.all_to_all(
-        dispatch(jnp.repeat(tokens, route_count, axis=0)),
-        "expert",
-        split_axis=0,
-        concat_axis=0,
-        tiled=True,
-    )
+    def exchange(buffer):
+        return lax.all_to_all(buffer, "expert", split_axis=0, concat_axis=0, tiled=True)
+
+    sent_rows = exchange(to_slots(token_onehot, tokens))
     preact = jnp.einsum("sekd,deh->sekh", sent_rows, w_in, preferred_element_type=jnp.float32)
     activation = swiglu_forward(preact, hidden).astype(jnp.bfloat16)
     outputs = jnp.einsum(
         "sekh,hed->sekd", activation, w_out, preferred_element_type=jnp.float32
     ).astype(jnp.bfloat16)
-    returned = lax.all_to_all(outputs, "expert", split_axis=0, concat_axis=0, tiled=True)
-    route_rows = returned.reshape(experts_all * capacity, model_width)[slot_index]
+    returned = exchange(outputs).reshape(slot_total, model_width)
+    route_rows = jnp.dot(route_onehot, returned, preferred_element_type=jnp.float32)
     student = tokens.astype(jnp.float32) + jnp.sum(
-        route_rows.astype(jnp.float32).reshape(tok_rows, route_count, model_width)
-        * weights_flat.reshape(tok_rows, route_count, 1),
-        axis=1,
+        route_rows.reshape(tok_rows, route_count, model_width) * gate_rows[:, :, None], axis=1
     )
     residual_grad = student - target.astype(jnp.float32)
-    scaled = (weights_flat * jnp.repeat(residual_grad, route_count, axis=0)).astype(jnp.bfloat16)
-    sent_grads = lax.all_to_all(dispatch(scaled), "expert", split_axis=0, concat_axis=0, tiled=True)
+    scaled = (gate_rows[:, :, None] * residual_grad[:, None, :]).astype(jnp.bfloat16)
+    sent_grads = exchange(to_slots(route_onehot, scaled.reshape(routes, model_width)))
     act_grad = jnp.einsum("sekd,hed->sekh", sent_grads, w_out, preferred_element_type=jnp.float32)
     pre_grad = swiglu_backward(preact, act_grad, hidden).astype(jnp.bfloat16)
     input_grads = jnp.einsum(
         "sekh,deh->sekd", pre_grad, w_in, preferred_element_type=jnp.float32
     ).astype(jnp.bfloat16)
-    returned_grads = lax.all_to_all(input_grads, "expert", split_axis=0, concat_axis=0, tiled=True)
-    route_back = returned_grads.reshape(experts_all * capacity, model_width)[slot_index]
+    returned_grads = exchange(input_grads).reshape(slot_total, model_width)
     grad_tokens = (
-        residual_grad
-        + jnp.sum(
-            route_back.astype(jnp.float32).reshape(tok_rows, route_count, model_width), axis=1
-        )
+        residual_grad + jnp.dot(token_onehot, returned_grads, preferred_element_type=jnp.float32)
     ).astype(jnp.bfloat16)
     term_in = jnp.einsum("sekd,sekh->deh", sent_rows, pre_grad, preferred_element_type=jnp.float32)
     term_out = jnp.einsum(

time: 522 us -> 444 us (0.85); the launches traced: 512 us -> 444 us
  local copies, waits for them, and re-layouts: 133 us -> 32.8 us
  waiting for transfers between devices: 95.1 us -> 137 us
  other arithmetic: 31.7 us -> 3.98 us
  matrix products: 69.7 us -> 79.5 us
  blocking collectives: 163 us -> 171 us
    reshape x8 -> x0, local copies, waits for them, and re-layouts: 43.9 us -> none  [the longest x4 23.2 us: dispatch(): return buffer.reshape(expert_peers, local_experts, capacity, model_width)]
    reduce_scatter x1, waiting for transfers between devices: 46.5 us -> 85 us  [per_device(): lax.psum_scatter(term_in.astype(jnp.bfloat16), 'dp', scatter_dimension=0,...]
    gather x2 -> x0, local copies, waits for them, and re-layouts: 18.5 us -> none  [the longest x1 9.54 us: per_device(): returned_grads.reshape(experts_all * capacity, model_width)[slot_index]]
    dot_general x0 -> x4, matrix products: none -> 16.4 us  [the longest x2 8.91 us: to_slots(): lax.dot_general(onehot, rows, (((0,), (0,)), ((), ())), preferred_element...]
    scatter x1 -> x0, other arithmetic: 14.6 us -> none  [dispatch(): buffer = jnp.zeros((experts_all * capacity, model_width), route_rows.dtyp...]
    reduce_sum x2 -> x1, other arithmetic: 12.5 us -> 0.39 us  [per_device(): jnp.sum(route_onehot.reshape(tok_rows, route_count, slot_total).astype(jn...]
    mul x3, local copies, waits for them, and re-layouts: 0.32 us -> 11.3 us  [the longest x2 11.2 us: per_device(): gate_rows[:, :, None] * residual_grad[:, None, :]]
    scatter x1 -> x0, local copies, waits for them, and re-layouts: 10.3 us -> none  [dispatch(): buffer = jnp.zeros((experts_all * capacity, model_width), route_rows.dtyp...]
  transfers between devices with their start and end apart: 3 -> 3, of which waited for: 2 -> 2; matrix products, arithmetic and copies ran while one was open for 16% -> 9% of each run, Pallas kernels for 0% -> 0%
where the time goes in v1:
time: 444 us
  blocking collectives  171 us (39%)
  waiting for transfers between devices  137 us (31%)
  matrix products  79.5 us (18%)
  local copies, waits for them, and re-layouts  32.8 us (7%)
  between operations  14.3 us (3%)
  starting transfers between devices  5.04 us (1%)
    all_to_all x3, blocking collectives, exchange(): lax.all_to_all(buffer, 'expert', split_axis=0, concat_axis=0, tiled=True)  171 us
    reduce_scatter x1, waiting for transfers between devices, per_device(): lax.psum_scatter(term_in.astype(jnp.bfloat16), 'dp', scatter_dimension=0,...  85 us
    all_to_all x1, waiting for transfers between devices, exchange(): lax.all_to_all(buffer, 'expert', split_axis=0, concat_axis=0, tiled=True)  51.7 us
    unnamed x26, local copies, waits for them, and re-layouts  17.7 us
    dot_general x1, matrix products, per_device(): jnp.einsum('sekd,deh->sekh', sent_rows, w_in, preferred_element_type=jnp....  12.4 us
    dot_general x1, matrix products, per_device(): jnp.einsum('sekh,hed->sekd', activation, w_out, preferred_element_type=jn...  12.4 us
    dot_general x1, matrix products, per_device(): jnp.einsum('sekd,hed->sekh', sent_grads, w_out, preferred_element_type=jn...  11.7 us
    dot_general x1, matrix products, per_device(): jnp.einsum('sekh,deh->sekd', pre_grad, w_in, preferred_element_type=jnp.f...  11.3 us
  transfers between devices with their start and end apart: 3, of which 2 were waited for; matrix products, arithmetic and copies ran while one was open for 9% of the time, Pallas kernels for 0%

profile of v1, /device:TPU:1, one launch (start us, length us, event | category | flops | bytes accessed | tf_op | source)
XLA Modules:
  0.0 443.5 jit_solution(3418467246259093782)
XLA Ops:
  7.2 0.8 copy.82
  8.0 0.1 eq.67
  8.1 0.1 eq.71
  8.2 1.5 reduce-window.6
  9.7 0.3 slice_reduce_fusion
  10.0 0.1 fusion.34
  10.1 0.1 reduce_sum.33
  10.2 0.1 copy.85
  10.3 0.7 multiply_add_fusion.1
  11.0 0.4 fusion.30
  11.4 0.0 copy-start.3
  11.4 2.5 convolution_convert_fusion.1
  14.0 59.0 %all_to_all.20 = bf16[32,2,16,2048]{3,2,1,0:T(8,128)(2,1)S(1)} all-to-all(bf16[32,2,16,2048]{3,2,1,0:T(8,128)(2,1)S(1)} %bitcast.64), channel_id=1, replica_groups=mesh['dp'=4,'expert'=32] {'expert'}, dimensions={0} | all-to-all | bytes 8388608 | tf_op jit(solution)/shard_map/all_to_all | solution.py:54
  73.0 12.4 %fusion.10 = f32[32,2,16,1536]{3,2,0,1:T(8,128)S(1)} fusion(bf16[2048,2,1536,1]{2,1,0,3:T(2,128)(2,1)} %bitcast.68, bf16[32,2,16,2048]{3,2,1,0:T(8,128)(2,1)S(1)} %all_to_all.20), kind=kOutput, calls=%fused_computation.14 | convolution fusion | flops 6442450944 | bytes 23068672 | tf_op jit(solution)/shard_map/sekd,deh->sekh/dot_general | solution.py:57
  85.4 1.0 multiply_convert_fusion.1
  86.4 12.4 %convert_bitcast_fusion.1 = bf16[32,2,16,2048]{3,2,0,1:T(8,128)(2,1)S(1)} fusion(bf16[32,2,16,768]{3,2,0,1:T(8,128)(2,1)S(1)} %multiply_convert_fusion.1, bf16[768,2,2048,1]{2,1,0,3:T(2,128)(2,1)} %bitcast.70), kind=kOutput, calls=%fused_computation.17 | convolution fusion | flops 3223322624 | bytes 12058624 | tf_op jit(solution)/shard_map/sekh,hed->sekd/dot_general | solution.py:59
  98.8 0.0 copy-done.2
  98.8 2.7 copy.89
  101.5 4.8 %all-to-all-start.1 = ((bf16[32,2,16,2048]{3,2,1,0:T(8,128)(2,1)}), bf16[32,2,16,2048]{3,2,1,0:T(8,128)(2,1)}, u32[]{:S(2)}, u32[]{:S(2)}) async-start(bf16[32,2,16,2048]{3,2,1,0:T(8,128)(2,1)} %copy.89), calls=%async_computation.1 | async-start | bytes 8388608 | tf_op jit(solution)/shard_map/all_to_all | solution.py:54
  106.3 0.2 reduce-scatter.5.cloned.1.call-start
  106.5 0.0 copy-done.10
  106.5 0.1 copy.90
  106.7 0.1 mul.75
  106.8 51.7 %all-to-all-done.1 = bf16[32,2,16,2048]{3,2,1,0:T(8,128)(2,1)} async-done(((bf16[32,2,16,2048]{3,2,1,0:T(8,128)(2,1)}), bf16[32,2,16,2048]{3,2,1,0:T(8,128)(2,1)}, u32[]{:S(2)}, u32[]{:S(2)}) %all-to-all-start.1) | async-done | bytes 4194336 | tf_op jit(solution)/shard_map/all_to_all | solution.py:54
  158.5 5.7 %multiply_reduce_fusion = f32[160,2048]{1,0:T(8,128)S(1)} fusion(bf16[1024,2048,1]{1,0,2:T(8,128)(2,1)} %bitcast.8, f32[160,4]{0,1:T(4,128)S(1)} %copy-done.10, s32[160,4]{0,1:T(4,128)S(1)} %multiply_add_fusion.1), kind=kOutput, calls=%fused_computation.13 | convolution fusion | flops 2687303680 | bytes 5510144 | tf_op jit(solution)/shard_map/dot_general | solution.py:63
  164.3 0.2 convert_subtract_fusion
  164.5 0.0 copy-start
  164.6 1.0 copy-done
  165.6 3.9 mul.77
  169.5 7.3 %mul.78 = f32[640,2048]{1,0:T(8,128)} reshape(f32[160,4,2048]{2,1,0:T(4,128)} %mul.77) | data formatting | bytes 10485760 | tf_op jit(solution)/shard_map/mul | solution.py:68
  176.8 6.4 %convolution_convert_fusion = bf16[1024,2048]{1,0:T(8,128)(2,1)S(1)} fusion(f32[640,2048]{1,0:T(8,128)} %mul.78, f32[640]{0:T(1024)S(1)} %mul.75, s32[640]{0:T(1024)S(1)} %multiply_add_fusion), kind=kOutput, calls=%fused_computation.18 | convolution fusion | flops 2689728512 | bytes 9442304 | tf_op jit(solution)/shard_map/dot_general | solution.py:48
  183.2 57.5 %all_to_all.21 = bf16[32,2,16,2048]{3,2,1,0:T(8,128)(2,1)S(1)} all-to-all(bf16[32,2,16,2048]{3,2,1,0:T(8,128)(2,1)S(1)} %bitcast.66), channel_id=1, replica_groups=mesh['dp'=4,'expert'=32] {'expert'}, dimensions={0} | all-to-all | bytes 8388608 | tf_op jit(solution)/shard_map/all_to_all | solution.py:54
  240.7 2.0 copy-done.7
  242.8 5.4 %fusion.5 = bf16[768,2,2048]{0,2,1:T(8,128)(2,1)} fusion(bf16[32,2,16,2048]{3,2,1,0:T(8,128)(2,1)S(1)} %all_to_all.21, bf16[32,2,16,768]{3,2,0,1:T(8,128)(2,1)S(1)} %multiply_convert_fusion.1), kind=kOutput, calls=%fused_computation.7 | convolution fusion | flops 3224371200 | bytes 12058624 | tf_op jit(solution)/shard_map/sekh,sekd->hed/dot_general | solution.py:80
  248.2 0.0 reduce-scatter.5.cloned.1.call-update
  248.2 0.0 reduce-scatter.3.cloned.1.call-start
  248.3 11.7 %fusion.21 = (bf16[32,2,16,768]{3,2,0,1:T(8,128)(2,1)S(1)}, bf16[32,2,16,768]{3,2,0,1:T(8,128)(2,1)S(1)}) fusion(f32[32,2,16,1536]{3,2,0,1:T(8,128)} %copy-done.2, bf16[768,2,2048,1]{2,1,0,3:T(2,128)(2,1)} %bitcast.71, bf16[32,2,16,2048]{3,2,1,0:T(8,128)(2,1)} %copy-done.7), kind=kOutput, calls=%fused_computation.26 | convolution fusion | flops 3231449088 | bytes 19922944 | tf_op jit(solution)/shard_map/sekd,hed->sekh/dot_general | solution.py:70
  259.9 9.9 %fusion.4 = bf16[2048,2,1536]{0,2,1:T(8,128)(2,1)} fusion(bf16[32,2,16,2048]{3,2,1,0:T(8,128)(2,1)S(1)} %copy-done.6, bf16[32,2,16,768]{3,2,0,1:T(8,128)(2,1)S(1)} %get-tuple-element.19, bf16[32,2,16,768]{3,2,0,1:T(8,128)(2,1)S(1)} %get-tuple-element.18), kind=kOutput, calls=%fused_computation.6 | convolution fusion | flops 6455033856 | bytes 19922944 | tf_op jit(solution)/shard_map/sekd,sekh->deh/dot_general | solution.py:79
  269.9 0.0 reduce-scatter.3.cloned.1.call-update
  269.9 11.3 %convert_bitcast_fusion = bf16[32,2,16,2048]{3,2,0,1:T(8,128)(2,1)S(1)} fusion(bf16[2048,2,1536,1]{2,1,0,3:T(2,128)(2,1)} %bitcast.69, bf16[32,2,16,768]{3,2,0,1:T(8,128)(2,1)S(1)} %get-tuple-element.19, bf16[32,2,16,768]{3,2,0,1:T(8,128)(2,1)S(1)} %get-tuple-element.18), kind=kOutput, calls=%fused_computation.16 | convolution fusion | flops 6450839552 | bytes 19922944 | tf_op jit(solution)/shard_map/sekh,deh->sekd/dot_general | solution.py:72
  281.2 0.5 copy.94
  281.7 0.0 copy-start.1
  281.7 0.0 copy-start.4
  281.7 54.5 %all_to_all.22 = bf16[32,2,16,2048]{3,2,1,0:T(8,128)(2,1)S(1)} all-to-all(bf16[32,2,16,2048]{3,2,1,0:T(8,128)(2,1)S(1)} %copy.94), channel_id=1, replica_groups=mesh['dp'=4,'expert'=32] {'expert'}, dimensions={0} | all-to-all | bytes 8388608 | tf_op jit(solution)/shard_map/all_to_all | solution.py:54
  336.3 1.7 fusion.28
  338.0 4.9 %copy.98 = bf16[768,2,512]{2,1,0:T(2,128)(2,1)} copy(bf16[768,2,512]{0,2,1:T(8,128)(2,1)} %reduce-scatter.5.cloned.1.call-done) | data formatting | bytes 3145728
  342.9 85.0 %reduce-scatter.3.cloned.1.call-done = bf16[512,2,1536]{0,2,1:T(8,128)(2,1)} async-done(((bf16[2048,2,1536]{0,2,1:T(8,128)(2,1)}), bf16[512,2,1536]{0,2,1:T(8,128)(2,1)}) %reduce-scatter.3.cloned.1.call-update) | async-done | bytes 3145744 | tf_op jit(solution)/shard_map/reduce_scatter | solution.py:84
  427.9 8.7 %copy.97 = bf16[512,2,1536]{2,1,0:T(2,128)(2,1)} copy(bf16[512,2,1536]{0,2,1:T(8,128)(2,1)} %reduce-scatter.3.cloned.1.call-done) | data formatting | bytes 6291456
  (18 shorter events, 0.1 us)
Async XLA Ops:
  11.4 2.5 copy-start.3
  73.0 12.4 %copy-start.5 = (bf16[32,2,16,2048]{3,2,1,0:T(8,128)(2,1)}, bf16[32,2,16,2048]{3,2,1,0:T(8,128)(2,1)S(1)}, u32[]{:S(2)}) copy-start(bf16[32,2,16,2048]{3,2,1,0:T(8,128)(2,1)S(1)} %all_to_all.20) | copy-start | bytes 12582916
  85.4 13.4 %copy-start.2 = (f32[32,2,16,1536]{3,2,0,1:T(8,128)}, f32[32,2,16,1536]{3,2,0,1:T(8,128)S(1)}, u32[]{:S(2)}) copy-start(f32[32,2,16,1536]{3,2,0,1:T(8,128)S(1)} %fusion.10) | copy-start | bytes 18874372
  101.5 5.0 %copy-start.10 = (f32[160,4]{0,1:T(4,128)S(1)}, f32[160,4]{0,1:T(4,128)}, u32[]{:S(2)}) copy-start(f32[160,4]{0,1:T(4,128)} %param.9) | copy-start | bytes 7684
  101.5 57.0 %all-to-all-start.1 = ((bf16[32,2,16,2048]{3,2,1,0:T(8,128)(2,1)}), bf16[32,2,16,2048]{3,2,1,0:T(8,128)(2,1)}, u32[]{:S(2)}, u32[]{:S(2)}) async-start(bf16[32,2,16,2048]{3,2,1,0:T(8,128)(2,1)} %copy.89), calls=%async_computation.1 | async-start | bytes 8388608 | tf_op jit(solution)/shard_map/all_to_all | solution.py:54
  106.3 231.7 %reduce-scatter.5.cloned.1.call-start = ((), (), s32[]{:S(2)}) async-start(), calls=%async_computation.7 | async-start | bytes 7864320 | tf_op jit(solution)/shard_map/reduce_scatter | solution.py:87
  158.5 5.7 %copy-start.8 = (bf16[160,2048]{1,0:T(8,128)(2,1)S(1)}, bf16[160,2048]{1,0:T(8,128)(2,1)}, u32[]{:S(2)}) copy-start(bf16[160,2048]{1,0:T(8,128)(2,1)} %param.6) | copy-start | bytes 1966084
  158.5 5.8 %copy-start.9 = (bf16[160,2048]{1,0:T(8,128)(2,1)S(1)}, bf16[160,2048]{1,0:T(8,128)(2,1)}, u32[]{:S(2)}) copy-start(bf16[160,2048]{1,0:T(8,128)(2,1)} %param.7) | copy-start | bytes 1966084
  164.5 1.1 copy-start
  240.7 2.0 copy-start.7
  248.2 179.7 %reduce-scatter.3.cloned.1.call-start = ((), (), s32[]{:S(2)}) async-start(), calls=%async_computation.6 | async-start | bytes 15728640 | tf_op jit(solution)/shard_map/reduce_scatter | solution.py:84
  248.2 11.7 %copy-start.6 = (bf16[32,2,16,2048]{3,2,1,0:T(8,128)(2,1)S(1)}, bf16[32,2,16,2048]{3,2,1,0:T(8,128)(2,1)}, u32[]{:S(2)}) copy-start(bf16[32,2,16,2048]{3,2,1,0:T(8,128)(2,1)} %copy-done.5) | copy-start | bytes 12582916
  281.7 54.6 %copy-start.1 = (f32[160,2048]{1,0:T(8,128)S(1)}, f32[160,2048]{1,0:T(8,128)}, u32[]{:S(2)}) copy-start(f32[160,2048]{1,0:T(8,128)} %copy-done) | copy-start | bytes 3932164
  281.7 54.6 %copy-start.4 = (bf16[160,1024]{1,0:T(8,128)(2,1)S(1)}, bf16[160,1024]{1,0:T(8,128)(2,1)}, u32[]{:S(2)}) copy-start(bf16[160,1024]{1,0:T(8,128)(2,1)} %copy-done.3) | copy-start | bytes 983044
Sparse Core Ops, SparseCore 0:
  248.3 62.7 reduce-scatter.4
  313.6 114.2 reduce-scatter.2

commit v2 on v1

--- a/solution.py
+++ b/solution.py
@@ -30,7 +30,7 @@
     slots_per = -(-capacity // 16) * 16
     slot_total = experts_all * slots_per
     routes = tok_rows * route_count
-    flat_ids = expert_ids.reshape(routes)
+    flat_ids = expert_ids.T.reshape(routes)
     matches = (flat_ids[:, None] == jnp.arange(experts_all, dtype=jnp.int32)[None, :]).astype(
         jnp.int32
     )
@@ -40,9 +40,9 @@
         jnp.bfloat16
     )
     token_onehot = jnp.sum(
-        route_onehot.reshape(tok_rows, route_count, slot_total).astype(jnp.float32), axis=1
+        route_onehot.reshape(route_count, tok_rows, slot_total).astype(jnp.float32), axis=0
     ).astype(jnp.bfloat16)
-    gate_rows = gates.reshape(tok_rows, route_count)
+    gate_rows = gates.T
 
     def to_slots(onehot, rows):
         buffer = lax.dot_general(
@@ -62,10 +62,10 @@
     returned = exchange(outputs).reshape(slot_total, model_width)
     route_rows = jnp.dot(route_onehot, returned, preferred_element_type=jnp.float32)
     student = tokens.astype(jnp.float32) + jnp.sum(
-        route_rows.reshape(tok_rows, route_count, model_width) * gate_rows[:, :, None], axis=1
+        route_rows.reshape(route_count, tok_rows, model_width) * gate_rows[:, :, None], axis=0
     )
     residual_grad = student - target.astype(jnp.float32)
-    scaled = (gate_rows[:, :, None] * residual_grad[:, None, :]).astype(jnp.bfloat16)
+    scaled = (gate_rows[:, :, None] * residual_grad[None, :, :]).astype(jnp.bfloat16)
     sent_grads = exchange(to_slots(route_onehot, scaled.reshape(routes, model_width)))
     act_grad = jnp.einsum("sekd,hed->sekh", sent_grads, w_out, preferred_element_type=jnp.float32)
     pre_grad = swiglu_backward(preact, act_grad, hidden).astype(jnp.bfloat16)

time: 444 us -> 431 us (0.971)
  local copies, waits for them, and re-layouts: 32.8 us -> 22.4 us
    mul x3 -> x1, local copies, waits for them, and re-layouts: 11.3 us -> 0.08 us  [per_device(): route_rows.reshape(route_count, tok_rows, model_width)]
    unnamed x26 -> x24, local copies, waits for them, and re-layouts: 17.7 us -> 17.4 us
where the time goes in v2:
time: 431 us; the launch traced here: 430 us
  blocking collectives  171 us (40%)
  waiting for transfers between devices  137 us (32%)
  matrix products  75.9 us (18%)
  local copies, waits for them, and re-layouts  22.4 us (5%)
  between operations  14.3 us (3%)
  starting transfers between devices  5.04 us (1%)
    all_to_all x3, blocking collectives, exchange(): lax.all_to_all(buffer, 'expert', split_axis=0, concat_axis=0, tiled=True)  171 us
    reduce_scatter x1, waiting for transfers between devices, per_device(): lax.psum_scatter(term_in.astype(jnp.bfloat16), 'dp', scatter_dimension=0,...  85 us
    all_to_all x1, waiting for transfers between devices, exchange(): lax.all_to_all(buffer, 'expert', split_axis=0, concat_axis=0, tiled=True)  51.9 us
    unnamed x24, local copies, waits for them, and re-layouts  17.4 us
    dot_general x1, matrix products, per_device(): jnp.einsum('sekd,deh->sekh', sent_rows, w_in, preferred_element_type=jnp....  12.5 us
    dot_general x1, matrix products, per_device(): jnp.einsum('sekd,hed->sekh', sent_grads, w_out, preferred_element_type=jn...  11.7 us
    dot_general x1, matrix products, per_device(): jnp.einsum('sekh,deh->sekd', pre_grad, w_in, preferred_element_type=jnp.f...  11.3 us
    dot_general x1, matrix products, per_device(): jnp.einsum('sekh,hed->sekd', activation, w_out, preferred_element_type=jn...  11.2 us
  transfers between devices with their start and end apart: 3, of which 2 were waited for; matrix products, arithmetic and copies ran while one was open for 9% of the time, Pallas kernels for 0%

profile of v2, /device:TPU:1, one launch (start us, length us, event | category | flops | bytes accessed | tf_op | source)
XLA Modules:
  0.0 429.9 jit_solution(5404145371410481633)
XLA Ops:
  7.2 0.8 eq.67
  7.9 0.8 eq.71
  8.7 1.5 reduce-window.6
  10.2 0.3 slice_reduce_fusion
  10.5 0.1 fusion.34
  10.7 0.1 reduce_sum.33
  10.7 0.7 multiply_add_fusion.1
  11.4 0.4 fusion.30
  11.8 0.0 copy-start.3
  11.8 2.5 convolution_convert_fusion.1
  14.3 0.0 copy-done.3
  14.4 59.0 %all_to_all.20 = bf16[32,2,16,2048]{3,2,1,0:T(8,128)(2,1)S(1)} all-to-all(bf16[32,2,16,2048]{3,2,1,0:T(8,128)(2,1)S(1)} %bitcast.72), channel_id=1, replica_groups=mesh['dp'=4,'expert'=32] {'expert'}, dimensions={0} | all-to-all | bytes 8388608 | tf_op jit(solution)/shard_map/all_to_all | solution.py:54
  73.4 12.5 %fusion.11 = f32[32,2,16,1536]{3,2,0,1:T(8,128)S(1)} fusion(bf16[2048,2,1536,1]{2,1,0,3:T(2,128)(2,1)} %bitcast.80, bf16[32,2,16,2048]{3,2,1,0:T(8,128)(2,1)S(1)} %all_to_all.20), kind=kOutput, calls=%fused_computation.15 | convolution fusion | flops 6442450944 | bytes 23068672 | tf_op jit(solution)/shard_map/sekd,deh->sekh/dot_general | solution.py:57
  85.8 0.0 copy-done.5
  85.8 0.0 copy-start.2
  85.8 1.0 multiply_convert_fusion
  86.8 1.7 copy-done.2
  88.5 11.2 %convert_bitcast_fusion.1 = bf16[32,2,16,2048]{3,2,0,1:T(8,128)(2,1)S(1)} fusion(bf16[32,2,16,768]{3,2,0,1:T(8,128)(2,1)S(1)} %multiply_convert_fusion, bf16[768,2,2048,1]{2,1,0,3:T(2,128)(2,1)} %bitcast.82), kind=kOutput, calls=%fused_computation.18 | convolution fusion | flops 3223322624 | bytes 12058624 | tf_op jit(solution)/shard_map/sekh,hed->sekd/dot_general | solution.py:59
  99.7 2.6 copy.53
  102.3 4.8 %all-to-all-start.1 = ((bf16[32,2,16,2048]{3,2,1,0:T(8,128)(2,1)}), bf16[32,2,16,2048]{3,2,1,0:T(8,128)(2,1)}, u32[]{:S(2)}, u32[]{:S(2)}) async-start(bf16[32,2,16,2048]{3,2,1,0:T(8,128)(2,1)} %copy.53), calls=%async_computation.1 | async-start | bytes 8388608 | tf_op jit(solution)/shard_map/all_to_all | solution.py:54
  107.1 0.2 reduce-scatter.5.cloned.1.call-start
  107.3 0.0 copy-done.10
  107.3 0.1 mul.75
  107.4 51.9 %all-to-all-done.1 = bf16[32,2,16,2048]{3,2,1,0:T(8,128)(2,1)} async-done(((bf16[32,2,16,2048]{3,2,1,0:T(8,128)(2,1)}), bf16[32,2,16,2048]{3,2,1,0:T(8,128)(2,1)}, u32[]{:S(2)}, u32[]{:S(2)}) %all-to-all-start.1) | async-done | bytes 4194336 | tf_op jit(solution)/shard_map/all_to_all | solution.py:54
  159.3 5.7 %multiply_reduce_fusion = f32[160,2048]{1,0:T(8,128)S(1)} fusion(bf16[1024,2048,1]{1,0,2:T(8,128)(2,1)} %bitcast.9, f32[4,160]{1,0:T(4,128)S(1)} %bitcast.79, s32[4,160]{1,0:T(4,128)S(1)} %multiply_add_fusion.1), kind=kOutput, calls=%fused_computation.14 | convolution fusion | flops 2687303680 | bytes 5510144 | tf_op jit(solution)/shard_map/dot_general | solution.py:63
  165.0 0.2 convert_subtract_fusion
  165.3 0.0 copy-start
  165.3 0.3 fusion.10
  165.6 4.0 convolution_convert_fusion
  169.6 57.6 %all_to_all.21 = bf16[32,2,16,2048]{3,2,1,0:T(8,128)(2,1)S(1)} all-to-all(bf16[32,2,16,2048]{3,2,1,0:T(8,128)(2,1)S(1)} %bitcast.74), channel_id=1, replica_groups=mesh['dp'=4,'expert'=32] {'expert'}, dimensions={0} | all-to-all | bytes 8388608 | tf_op jit(solution)/shard_map/all_to_all | solution.py:54
  227.2 2.0 copy-done.7
  229.2 5.4 %fusion.5 = bf16[768,2,2048]{0,2,1:T(8,128)(2,1)} fusion(bf16[32,2,16,2048]{3,2,1,0:T(8,128)(2,1)S(1)} %all_to_all.21, bf16[32,2,16,768]{3,2,0,1:T(8,128)(2,1)S(1)} %multiply_convert_fusion), kind=kOutput, calls=%fused_computation.7 | convolution fusion | flops 3224371200 | bytes 12058624 | tf_op jit(solution)/shard_map/sekh,sekd->hed/dot_general | solution.py:80
  234.6 0.0 reduce-scatter.5.cloned.1.call-update
  234.6 0.0 reduce-scatter.3.cloned.1.call-start
  234.7 0.0 copy-start.6
  234.7 11.7 %fusion.22 = (bf16[32,2,16,768]{3,2,0,1:T(8,128)(2,1)S(1)}, bf16[32,2,16,768]{3,2,0,1:T(8,128)(2,1)S(1)}) fusion(f32[32,2,16,1536]{3,2,0,1:T(8,128)} %copy-done.2, bf16[768,2,2048,1]{2,1,0,3:T(2,128)(2,1)} %bitcast.83, bf16[32,2,16,2048]{3,2,1,0:T(8,128)(2,1)} %copy-done.7), kind=kOutput, calls=%fused_computation.27 | convolution fusion | flops 3231449088 | bytes 19922944 | tf_op jit(solution)/shard_map/sekd,hed->sekh/dot_general | solution.py:70
  246.4 9.9 %fusion.4 = bf16[2048,2,1536]{0,2,1:T(8,128)(2,1)} fusion(bf16[32,2,16,2048]{3,2,1,0:T(8,128)(2,1)S(1)} %copy-done.6, bf16[32,2,16,768]{3,2,0,1:T(8,128)(2,1)S(1)} %get-tuple-element.16, bf16[32,2,16,768]{3,2,0,1:T(8,128)(2,1)S(1)} %get-tuple-element.15), kind=kOutput, calls=%fused_computation.6 | convolution fusion | flops 6455033856 | bytes 19922944 | tf_op jit(solution)/shard_map/sekd,sekh->deh/dot_general | solution.py:79
  256.3 0.0 reduce-scatter.3.cloned.1.call-update
  256.3 11.3 %convert_bitcast_fusion = bf16[32,2,16,2048]{3,2,0,1:T(8,128)(2,1)S(1)} fusion(bf16[2048,2,1536,1]{2,1,0,3:T(2,128)(2,1)} %bitcast.81, bf16[32,2,16,768]{3,2,0,1:T(8,128)(2,1)S(1)} %get-tuple-element.16, bf16[32,2,16,768]{3,2,0,1:T(8,128)(2,1)S(1)} %get-tuple-element.15), kind=kOutput, calls=%fused_computation.17 | convolution fusion | flops 6450839552 | bytes 19922944 | tf_op jit(solution)/shard_map/sekh,deh->sekd/dot_general | solution.py:72
  267.6 0.5 copy.57
  268.2 0.0 copy-start.1
  268.2 0.0 copy-start.4
  268.2 54.5 %all_to_all.22 = bf16[32,2,16,2048]{3,2,1,0:T(8,128)(2,1)S(1)} all-to-all(bf16[32,2,16,2048]{3,2,1,0:T(8,128)(2,1)S(1)} %copy.57), channel_id=1, replica_groups=mesh['dp'=4,'expert'=32] {'expert'}, dimensions={0} | all-to-all | bytes 8388608 | tf_op jit(solution)/shard_map/all_to_all | solution.py:54
  322.7 0.0 copy-done.1
  322.7 1.7 fusion.28
  324.4 4.9 %copy.61 = bf16[768,2,512]{2,1,0:T(2,128)(2,1)} copy(bf16[768,2,512]{0,2,1:T(8,128)(2,1)} %reduce-scatter.5.cloned.1.call-done) | data formatting | bytes 3145728
  329.3 85.0 %reduce-scatter.3.cloned.1.call-done = bf16[512,2,1536]{0,2,1:T(8,128)(2,1)} async-done(((bf16[2048,2,1536]{0,2,1:T(8,128)(2,1)}), bf16[512,2,1536]{0,2,1:T(8,128)(2,1)}) %reduce-scatter.3.cloned.1.call-update) | async-done | bytes 3145744 | tf_op jit(solution)/shard_map/reduce_scatter | solution.py:84
  414.4 8.7 %copy.60 = bf16[512,2,1536]{2,1,0:T(2,128)(2,1)} copy(bf16[512,2,1536]{0,2,1:T(8,128)(2,1)} %reduce-scatter.3.cloned.1.call-done) | data formatting | bytes 6291456
  (14 shorter events, 0.1 us)
Async XLA Ops:
  11.8 2.5 copy-start.3
  73.4 12.5 %copy-start.5 = (bf16[32,2,16,2048]{3,2,1,0:T(8,128)(2,1)}, bf16[32,2,16,2048]{3,2,1,0:T(8,128)(2,1)S(1)}, u32[]{:S(2)}) copy-start(bf16[32,2,16,2048]{3,2,1,0:T(8,128)(2,1)S(1)} %all_to_all.20) | copy-start | bytes 12582916
  85.8 2.7 copy-start.2
  102.3 5.0 %copy-start.10 = (f32[160,4]{0,1:T(4,128)S(1)}, f32[160,4]{0,1:T(4,128)}, u32[]{:S(2)}) copy-start(f32[160,4]{0,1:T(4,128)} %param.9) | copy-start | bytes 7684
  102.3 57.0 %all-to-all-start.1 = ((bf16[32,2,16,2048]{3,2,1,0:T(8,128)(2,1)}), bf16[32,2,16,2048]{3,2,1,0:T(8,128)(2,1)}, u32[]{:S(2)}, u32[]{:S(2)}) async-start(bf16[32,2,16,2048]{3,2,1,0:T(8,128)(2,1)} %copy.53), calls=%async_computation.1 | async-start | bytes 8388608 | tf_op jit(solution)/shard_map/all_to_all | solution.py:54
  107.1 217.4 %reduce-scatter.5.cloned.1.call-start = ((), (), s32[]{:S(2)}) async-start(), calls=%async_computation.7 | async-start | bytes 7864320 | tf_op jit(solution)/shard_map/reduce_scatter | solution.py:87
  159.3 5.7 %copy-start.8 = (bf16[160,2048]{1,0:T(8,128)(2,1)S(1)}, bf16[160,2048]{1,0:T(8,128)(2,1)}, u32[]{:S(2)}) copy-start(bf16[160,2048]{1,0:T(8,128)(2,1)} %param.6) | copy-start | bytes 1966084
  159.3 5.8 %copy-start.9 = (bf16[160,2048]{1,0:T(8,128)(2,1)S(1)}, bf16[160,2048]{1,0:T(8,128)(2,1)}, u32[]{:S(2)}) copy-start(bf16[160,2048]{1,0:T(8,128)(2,1)} %param.7) | copy-start | bytes 1966084
  165.3 4.3 %copy-start = (f32[160,2048]{1,0:T(8,128)}, f32[160,2048]{1,0:T(8,128)S(1)}, u32[]{:S(2)}) copy-start(f32[160,2048]{1,0:T(8,128)S(1)} %convert_subtract_fusion) | copy-start | bytes 3932164
  227.2 2.0 copy-start.7
  234.6 179.7 %reduce-scatter.3.cloned.1.call-start = ((), (), s32[]{:S(2)}) async-start(), calls=%async_computation.6 | async-start | bytes 15728640 | tf_op jit(solution)/shard_map/reduce_scatter | solution.py:84
  234.7 11.7 %copy-start.6 = (bf16[32,2,16,2048]{3,2,1,0:T(8,128)(2,1)S(1)}, bf16[32,2,16,2048]{3,2,1,0:T(8,128)(2,1)}, u32[]{:S(2)}) copy-start(bf16[32,2,16,2048]{3,2,1,0:T(8,128)(2,1)} %copy-done.5) | copy-start | bytes 12582916
  268.2 54.6 %copy-start.1 = (f32[160,2048]{1,0:T(8,128)S(1)}, f32[160,2048]{1,0:T(8,128)}, u32[]{:S(2)}) copy-start(f32[160,2048]{1,0:T(8,128)} %copy-done) | copy-start | bytes 3932164
  268.2 54.6 %copy-start.4 = (bf16[160,1024]{1,0:T(8,128)(2,1)S(1)}, bf16[160,1024]{1,0:T(8,128)(2,1)}, u32[]{:S(2)}) copy-start(bf16[160,1024]{1,0:T(8,128)(2,1)} %copy-done.3) | copy-start | bytes 983044
Sparse Core Ops, SparseCore 0:
  234.8 62.7 reduce-scatter.4
  300.0 114.2 reduce-scatter.2

commit v3 on v2

--- a/solution.py
+++ b/solution.py
@@ -76,19 +76,44 @@
     grad_tokens = (
         residual_grad + jnp.dot(token_onehot, returned_grads, preferred_element_type=jnp.float32)
     ).astype(jnp.bfloat16)
-    term_in = jnp.einsum("sekd,sekh->deh", sent_rows, pre_grad, preferred_element_type=jnp.float32)
+    peers = lax.axis_size("dp")
+    chunk_in = model_width // peers
+    term_in = jnp.einsum(
+        "sekcfd,sekh->cfdeh",
+        sent_rows.reshape(sent_rows.shape[:3] + (peers, 2, chunk_in // 2)),
+        pre_grad,
+        preferred_element_type=jnp.float32,
+    ).astype(jnp.bfloat16)
     term_out = jnp.einsum(
-        "sekh,sekd->hed", activation, sent_grads, preferred_element_type=jnp.float32
-    )
-    grad_in, grad_out = (
-        lax.psum_scatter(
-            term_in.astype(jnp.bfloat16), "dp", scatter_dimension=0, tiled=True
-        ).astype(jnp.float32),
-        lax.psum_scatter(
-            term_out.astype(jnp.bfloat16), "dp", scatter_dimension=2, tiled=True
-        ).astype(jnp.float32),
-    )
-    return (grad_tokens, grad_in.astype(jnp.bfloat16), grad_out.astype(jnp.bfloat16))
+        "sekfh,sekcd->cfhed",
+        activation.reshape(activation.shape[:3] + (2, hidden // 2)),
+        sent_grads.reshape(sent_grads.shape[:3] + (peers, chunk_in)),
+        preferred_element_type=jnp.float32,
+    ).astype(jnp.bfloat16)
+    grad_in = ring_reduce_scatter(term_in)
+    grad_out = ring_reduce_scatter(term_out)
+    return (grad_tokens, grad_in, grad_out)
+
+
+def ring_reduce_scatter(chunks):
+    peers = lax.axis_size("dp")
+    me = lax.axis_index("dp")
+    forward = [(i, (i + 1) % peers) for i in range(peers)]
+    backward = [(i, (i - 1) % peers) for i in range(peers)]
+
+    def own(offset, direction):
+        index = lax.rem(me + offset + peers, peers)
+        return lax.dynamic_index_in_dim(chunks, index, 0, keepdims=False)[direction]
+
+    def add(left, right):
+        return (left.astype(jnp.float32) + right.astype(jnp.float32)).astype(jnp.bfloat16)
+
+    up = lax.ppermute(own(-1, 0), "dp", forward)
+    down = lax.ppermute(own(1, 1), "dp", backward)
+    for step in range(2, peers):
+        up = lax.ppermute(add(up, own(-step, 0)), "dp", forward)
+        down = lax.ppermute(add(down, own(step, 1)), "dp", backward)
+    return jnp.concatenate([add(up, own(0, 0)), add(down, own(0, 1))], axis=0)
 
 
 def solution(mesh):

time: 431 us -> 451 us (1.046)
  the two profiles are of different devices: /device:TPU:1 before, /device:TPU:8 now
where the time goes in v3:
time: 451 us; the launch traced here: 443 us
  waiting for transfers between devices  182 us (40%)
  matrix products  88.1 us (20%)
  local copies, waits for them, and re-layouts  59.7 us (13%)
  blocking collectives  56.6 us (13%)
  starting transfers between devices  37.6 us (8%)
  other arithmetic  17.6 us (4%)
    all_to_all x3, waiting for transfers between devices, exchange(): lax.all_to_all(buffer, 'expert', split_axis=0, concat_axis=0, tiled=True)  100 us
    ppermute x4, waiting for transfers between devices, ring_reduce_scatter(): up = lax.ppermute(add(up, own(-step, 0)), 'dp', forward)  73.3 us
    all_to_all x1, blocking collectives, exchange(): lax.all_to_all(buffer, 'expert', split_axis=0, concat_axis=0, tiled=True)  56.6 us
    all_to_all x3, starting transfers between devices, exchange(): lax.all_to_all(buffer, 'expert', split_axis=0, concat_axis=0, tiled=True)  16.8 us
    unnamed x46, local copies, waits for them, and re-layouts  16.7 us
    another operation x2, local copies, waits for them, and re-layouts  15.4 us
    ppermute x4, starting transfers between devices, ring_reduce_scatter(): down = lax.ppermute(add(down, own(step, 1)), 'dp', backward)  13.2 us
    convert_element_type x10, other arithmetic, add(): (left.astype(jnp.float32) + right.astype(jnp.float32)).astype(jnp.bfloat16)  13 us
  transfers between devices with their start and end apart: 15, of which 7 were waited for; matrix products, arithmetic and copies ran while one was open for 19% of the time, Pallas kernels for 0%

profile of v3, /device:TPU:8, one launch (start us, length us, event | category | flops | bytes accessed | tf_op | source)
XLA Modules:
  0.0 442.9 jit_solution(10452970989666970322)
XLA Ops:
  2.2 1.5 reduce-window.6
  5.3 2.4 convolution_convert_fusion.1
  7.7 56.6 %all_to_all.20 = bf16[32,2,16,2048]{3,2,1,0:T(8,128)(2,1)S(1)} all-to-all(bf16[32,2,16,2048]{3,2,1,0:T(8,128)(2,1)S(1)} %bitcast.187), channel_id=1, replica_groups=mesh['dp'=4,'expert'=32] {'expert'}, dimensions={0} | all-to-all | bytes 8388608 | tf_op jit(solution)/shard_map/all_to_all | solution.py:54
  64.3 12.4 %fusion.9 = f32[32,2,16,1536]{3,2,0,1:T(8,128)S(1)} fusion(bf16[2048,2,1536,1]{2,1,0,3:T(2,128)(2,1)} %bitcast.208, bf16[32,2,16,2048]{3,2,1,0:T(8,128)(2,1)S(1)} %all_to_all.20), kind=kOutput, calls=%fused_computation.13 | convolution fusion | flops 6442450944 | bytes 23068672 | tf_op jit(solution)/shard_map/sekd,deh->sekh/dot_general | solution.py:57
  77.7 1.7 copy-done.9
  79.4 11.2 %convert_bitcast_fusion.1 = bf16[32,2,16,2048]{3,2,0,1:T(8,128)(2,1)S(1)} fusion(bf16[32,2,16,768]{3,2,0,1:T(8,128)(2,1)S(1)} %multiply_convert_fusion, bf16[768,2,2048,1]{2,1,0,3:T(2,128)(2,1)} %bitcast.210), kind=kOutput, calls=%fused_computation.19 | convolution fusion | flops 3223322624 | bytes 12058624 | tf_op jit(solution)/shard_map/sekh,hed->sekd/dot_general | solution.py:59
  90.6 2.7 copy.114
  93.3 6.7 %all-to-all-start.1 = ((bf16[32,2,16,2048]{3,2,1,0:T(8,128)(2,1)}), bf16[32,2,16,2048]{3,2,1,0:T(8,128)(2,1)}, u32[]{:S(2)}, u32[]{:S(2)}) async-start(bf16[32,2,16,2048]{3,2,1,0:T(8,128)(2,1)} %copy.114), calls=%async_computation.1 | async-start | bytes 8388608 | tf_op jit(solution)/shard_map/all_to_all | solution.py:54
  100.1 53.9 %all-to-all-done.1 = bf16[32,2,16,2048]{3,2,1,0:T(8,128)(2,1)} async-done(((bf16[32,2,16,2048]{3,2,1,0:T(8,128)(2,1)}), bf16[32,2,16,2048]{3,2,1,0:T(8,128)(2,1)}, u32[]{:S(2)}, u32[]{:S(2)}) %all-to-all-start.1) | async-done | bytes 4194336 | tf_op jit(solution)/shard_map/all_to_all | solution.py:54
  154.1 5.8 %multiply_reduce_fusion = f32[160,2048]{1,0:T(8,128)S(1)} fusion(bf16[1024,2048,1]{1,0,2:T(8,128)(2,1)} %bitcast.9, f32[4,160]{1,0:T(4,128)S(1)} %bitcast.207, s32[4,160]{1,0:T(4,128)S(1)} %multiply_add_fusion.1), kind=kOutput, calls=%fused_computation.12 | convolution fusion | flops 2687303680 | bytes 5510144 | tf_op jit(solution)/shard_map/dot_general | solution.py:63
  160.5 5.3 %convolution_convert_fusion = bf16[1024,2048]{1,0:T(8,128)(2,1)} fusion(bf16[640,2048]{1,0:T(8,128)(2,1)S(1)} %fusion.8, s32[640]{0:T(1024)S(1)} %multiply_add_fusion), kind=kOutput, calls=%fused_computation.20 | convolution fusion | flops 2687107072 | bytes 6818304 | tf_op jit(solution)/shard_map/dot_general | solution.py:48
  165.8 5.2 %all-to-all-start.2 = ((bf16[32,2,16,2048]{3,2,1,0:T(8,128)(2,1)}), bf16[32,2,16,2048]{3,2,1,0:T(8,128)(2,1)}, u32[]{:S(2)}, u32[]{:S(2)}) async-start(bf16[32,2,16,2048]{3,2,1,0:T(8,128)(2,1)} %bitcast.195), calls=%async_computation.2 | async-start | bytes 8388608 | tf_op jit(solution)/shard_map/all_to_all | solution.py:54
  171.5 7.8 %reshape.155 = bf16[32,2,16,4,2,256]{5,4,3,2,1,0:T(2,128)(2,1)} reshape(bf16[32,2,16,2048]{3,2,1,0:T(8,128)(2,1)} %copy-done) | data formatting | bytes 8388608 | tf_op jit(solution)/shard_map/reshape | solution.py:83
  179.3 46.3 %all-to-all-done.2 = bf16[32,2,16,2048]{3,2,1,0:T(8,128)(2,1)} async-done(((bf16[32,2,16,2048]{3,2,1,0:T(8,128)(2,1)}), bf16[32,2,16,2048]{3,2,1,0:T(8,128)(2,1)}, u32[]{:S(2)}, u32[]{:S(2)}) %all-to-all-start.2) | async-done | bytes 4194336 | tf_op jit(solution)/shard_map/all_to_all | solution.py:54
  225.6 7.8 %reshape.156 = bf16[32,2,16,4,512]{4,3,2,1,0:T(4,128)(2,1)} reshape(bf16[32,2,16,2048]{3,2,1,0:T(8,128)(2,1)} %all-to-all-done.2) | data formatting | bytes 8388608 | tf_op jit(solution)/shard_map/reshape | solution.py:90
  233.4 10.5 %bitcast_convert_fusion.1 = bf16[2,4,512,2,384]{2,4,3,1,0:T(8,128)(2,1)S(1)} fusion(bf16[32,2,16,4,512,1]{4,3,2,1,0,5:T(4,128)(2,1)} %bitcast.196, bf16[32,2,16,2,384,1]{4,3,2,0,1,5:T(2,128)(2,1)S(1)} %bitcast.202), kind=kOutput, calls=%fused_computation.1 | convolution fusion | flops 3224371200 | bytes 12058624 | tf_op jit(solution)/shard_map/sekfh,sekcd->cfhed/dot_general | solution.py:87
  243.9 3.3 constant_dynamic-slice_fusion.3
  248.2 4.0 collective-permute-start.9
  253.5 12.8 %fusion.28 = (bf16[32,2,16,768]{3,2,0,1:T(8,128)(2,1)S(1)}, bf16[32,2,16,768]{3,2,0,1:T(8,128)(2,1)}) fusion(f32[32,2,16,1536]{3,2,0,1:T(8,128)} %copy-done.9, bf16[768,2,2048,1]{2,1,0,3:T(2,128)(2,1)} %bitcast.211, bf16[32,2,16,2048]{3,2,1,0:T(8,128)(2,1)} %all-to-all-done.2), kind=kOutput, calls=%fused_computation.46 | convolution fusion | flops 3231449088 | bytes 19922944 | tf_op jit(solution)/shard_map/sekd,hed->sekh/dot_general | solution.py:70
  267.5 11.1 %bitcast_convert_fusion = bf16[2,1536,4,2,256]{1,4,3,2,0:T(8,128)(2,1)} fusion(bf16[32,2,16,4,2,256]{5,4,3,2,1,0:T(2,128)(2,1)S(1)} %copy-done.10, bf16[32,2,16,768]{3,2,0,1:T(8,128)(2,1)} %get-tuple-element.26, bf16[32,2,16,768]{3,2,0,1:T(8,128)(2,1)S(1)} %get-tuple-element.25), kind=kOutput, calls=%fused_computation | convolution fusion | flops 6455033856 | bytes 19922944 | tf_op jit(solution)/shard_map/sekcfd,sekh->cfdeh/dot_general | solution.py:81
  278.6 12.1 %constant_dynamic-slice_fusion.9 = (bf16[2,1536,1,2,256]{1,4,3,2,0:T(8,128)(2,1)S(1)}, bf16[2,1536,1,2,256]{1,4,3,2,0:T(8,128)(2,1)S(1)}, bf16[2,1536,1,2,256]{1...) fusion(bf16[2,1536,4,2,256]{1,4,3,2,0:T(8,128)(2,1)} %bitcast_c, ...), kind=kLoop, calls=%fused_computation.119 | loop fusion | bytes 44040220 | tf_op jit(solution)/shard_map/dynamic-slice.2
  291.0 1.3 slice_bitcast_fusion.3
  292.3 2.9 collective-permute-start.3
  295.4 1.2 slice_bitcast_fusion.7
  296.9 12.2 %convert_bitcast_fusion = bf16[32,2,16,2048]{3,2,0,1:T(8,128)(2,1)S(1)} fusion(bf16[2048,2,1536,1]{2,1,0,3:T(2,128)(2,1)} %bitcast.209, bf16[32,2,16,768]{3,2,0,1:T(8,128)(2,1)} %get-tuple-element.26, bf16[32,2,16,768]{3,2,0,1:T(8,128)(2,1)} %copy-done.15), kind=kOutput, calls=%fused_computation.18 | convolution fusion | flops 6450839552 | bytes 19922944 | tf_op jit(solution)/shard_map/sekh,deh->sekd/dot_general | solution.py:72
  309.1 2.5 copy.118
  311.6 4.8 %all-to-all-start.3 = ((bf16[32,2,16,2048]{3,2,1,0:T(8,128)(2,1)}), bf16[32,2,16,2048]{3,2,1,0:T(8,128)(2,1)}, u32[]{:S(2)}, u32[]{:S(2)}) async-start(bf16[32,2,16,2048]{3,2,1,0:T(8,128)(2,1)} %copy.118), calls=%async_computation.3 | async-start | bytes 8388608 | tf_op jit(solution)/shard_map/all_to_all | solution.py:54
  316.5 1.7 copy.221
  319.5 1.7 copy-done.2
  321.4 1.3 fusion.40
  322.9 1.3 fusion.37
  324.2 3.3 collective-permute-start.10
  327.6 8.2 %collective-permute-done = bf16[256,2,1536]{2,0,1:T(8,128)(2,1)} collective-permute-done((bf16[256,2,1536]{2,0,1:T(8,128)(2,1)}, bf16[256,2,1536]{2,0,1:T(8,128)(2,1)}, u32[]{:S(2)}, u32[]{:S(2)}) %collective-permute-start) | collective-permute-done | bytes 1572896 | tf_op jit(solution)/shard_map/ppermute | solution.py:111
  335.7 1.8 fusion.25
  337.6 1.9 fusion.22
  339.5 3.2 collective-permute-start.4
  343.0 9.4 %collective-permute-done.7 = bf16[384,2,512]{2,0,1:T(8,128)(2,1)S(1)} collective-permute-done((bf16[384,2,512]{2,0,1:T(8,128)(2,1)S(1)}, bf16[384,2,512]{2,0,1:T(8,128)(2,1)S(1)}, u32[]{:S(2)}, u32[]{:S(2)}) %collective-permute-start.7) | collective-permute-done | bytes 786464 | tf_op jit(solution)/shard_map/ppermute | solution.py:114
  353.0 3.3 collective-permute-start.11
  356.3 29.9 %collective-permute-done.1 = bf16[256,2,1536]{2,0,1:T(8,128)(2,1)S(1)} collective-permute-done((bf16[256,2,1536]{2,0,1:T(8,128)(2,1)S(1)}, bf16[256,2,1536]{2,0,1:T(8,128)(2,1)S(1)}, u32[]{:S(2)}, u32[]{:S(2)}) %collective-permute-start.1) | collective-permute-done | bytes 1572896 | tf_op jit(solution)/shard_map/ppermute | solution.py:114
  386.2 1.5 fusion.24
  387.7 1.5 fusion.21
  389.3 3.4 collective-permute-start.5
  393.0 10.0 %collective-permute-done.8 = bf16[384,2,512]{2,0,1:T(8,128)(2,1)S(1)} collective-permute-done((bf16[384,2,512]{2,0,1:T(8,128)(2,1)S(1)}, bf16[384,2,512]{2,0,1:T(8,128)(2,1)S(1)}, u32[]{:S(2)}, u32[]{:S(2)}) %collective-permute-start.8) | collective-permute-done | bytes 786464 | tf_op jit(solution)/shard_map/ppermute | solution.py:114
  403.6 2.8 copy.135
  406.4 4.3 fusion.34
  410.6 23.9 %collective-permute-done.2 = bf16[256,2,1536]{2,0,1:T(8,128)(2,1)} collective-permute-done((bf16[256,2,1536]{2,0,1:T(8,128)(2,1)}, bf16[256,2,1536]{2,0,1:T(8,128)(2,1)}, u32[]{:S(2)}, u32[]{:S(2)}) %collective-permute-start.2) | collective-permute-done | bytes 1572896 | tf_op jit(solution)/shard_map/ppermute | solution.py:114
  434.6 2.7 fusion.23
  437.5 4.9 %copy.134 = bf16[512,2,1536]{2,1,0:T(2,128)(2,1)} copy(bf16[512,2,1536]{2,0,1:T(8,128)(2,1)S(1)} %pad_maximum_fusion.1) | data formatting | bytes 6291456
  (77 shorter events, 12.8 us)
Async XLA Ops:
  64.3 12.5 %copy-start = (bf16[32,2,16,2048]{3,2,1,0:T(8,128)(2,1)}, bf16[32,2,16,2048]{3,2,1,0:T(8,128)(2,1)S(1)}, u32[]{:S(2)}) copy-start(bf16[32,2,16,2048]{3,2,1,0:T(8,128)(2,1)S(1)} %all_to_all.20) | copy-start | bytes 12582916
  76.7 2.7 copy-start.9
  93.3 6.8 %copy-start.14 = (f32[160,4]{0,1:T(4,128)S(1)}, f32[160,4]{0,1:T(4,128)}, u32[]{:S(2)}) copy-start(f32[160,4]{0,1:T(4,128)} %param.9) | copy-start | bytes 7684
  93.3 60.8 %all-to-all-start.1 = ((bf16[32,2,16,2048]{3,2,1,0:T(8,128)(2,1)}), bf16[32,2,16,2048]{3,2,1,0:T(8,128)(2,1)}, u32[]{:S(2)}, u32[]{:S(2)}) async-start(bf16[32,2,16,2048]{3,2,1,0:T(8,128)(2,1)} %copy.114), calls=%async_computation.1 | async-start | bytes 8388608 | tf_op jit(solution)/shard_map/all_to_all | solution.py:54
  154.1 5.8 %copy-start.12 = (bf16[160,2048]{1,0:T(8,128)(2,1)S(1)}, bf16[160,2048]{1,0:T(8,128)(2,1)}, u32[]{:S(2)}) copy-start(bf16[160,2048]{1,0:T(8,128)(2,1)} %param.6) | copy-start | bytes 1966084
  154.1 5.8 %copy-start.13 = (bf16[160,2048]{1,0:T(8,128)(2,1)S(1)}, bf16[160,2048]{1,0:T(8,128)(2,1)}, u32[]{:S(2)}) copy-start(bf16[160,2048]{1,0:T(8,128)(2,1)} %param.7) | copy-start | bytes 1966084
  160.1 5.7 %copy-start.4 = (f32[160,2048]{1,0:T(8,128)}, f32[160,2048]{1,0:T(8,128)S(1)}, u32[]{:S(2)}) copy-start(f32[160,2048]{1,0:T(8,128)S(1)} %convert_subtract_fusion) | copy-start | bytes 3932164
  165.8 59.8 %all-to-all-start.2 = ((bf16[32,2,16,2048]{3,2,1,0:T(8,128)(2,1)}), bf16[32,2,16,2048]{3,2,1,0:T(8,128)(2,1)}, u32[]{:S(2)}, u32[]{:S(2)}) async-start(bf16[32,2,16,2048]{3,2,1,0:T(8,128)(2,1)} %bitcast.195), calls=%async_computation.2 | async-start | bytes 8388608 | tf_op jit(solution)/shard_map/all_to_all | solution.py:54
  248.2 74.6 %collective-permute-start.9 = (bf16[384,2,512]{2,0,1:T(8,128)(2,1)}, bf16[384,2,512]{2,0,1:T(8,128)(2,1)}, u32[]{:S(2)}, u32[]{:S(2)}) collective-permute-start(bf16[384,2,512]{2,0,1:T(8,128)(2,1)} %slice_bitcast_fusion.11), channel_id=1, source_target_pairs={{0,96},{32,0},{64,32},{96,64},{1,97},{33,1},{65,33},{97,65},{2,98}... | collective-permute-start | bytes 2359304 | tf_op jit(solution)/shard_map/ppermute | solution.py:112
  253.3 14.2 %copy-start.10 = (bf16[32,2,16,4,2,256]{5,4,3,2,1,0:T(2,128)(2,1)S(1)}, bf16[32,2,16,4,2,256]{5,4,3,2,1,0:T(2,128)(2,1)}, u32[]{:S(2)}) copy-start(bf16[32,2,16,4,2,256]{5,4,3,2,1,0:T(2,128)(2,1)} %reshape.155) | copy-start | bytes 12582916
  253.3 68.1 %collective-permute-start.6 = (bf16[384,2,512]{2,0,1:T(8,128)(2,1)}, bf16[384,2,512]{2,0,1:T(8,128)(2,1)}, u32[]{:S(2)}, u32[]{:S(2)}) collective-permute-start(bf16[384,2,512]{2,0,1:T(8,128)(2,1)} %slice_bitcast_fusion.15), channel_id=1, source_target_pairs={{0,32},{32,64},{64,96},{96,0},{1,33},{33,65},{65,97},{97,1},{2,34}... | collective-permute-start | bytes 2359304 | tf_op jit(solution)/shard_map/ppermute | solution.py:111
  266.3 1.2 copy-start.15
  292.3 45.3 %collective-permute-start.3 = (bf16[256,2,1536]{2,0,1:T(8,128)(2,1)}, bf16[256,2,1536]{2,0,1:T(8,128)(2,1)}, u32[]{:S(2)}, u32[]{:S(2)}) collective-permute-start(bf16[256,2,1536]{2,0,1:T(8,128)(2,1)} %slice_bitcast_fusion.3), channel_id=1, source_target_pairs={{0,96},{32,0},{64,32},{96,64},{1,97},{33,1},{65,33},{97,65},{2,98}... | collective-permute-start | bytes 4718600 | tf_op jit(solution)/shard_map/ppermute | solution.py:112
  296.7 39.0 %collective-permute-start = (bf16[256,2,1536]{2,0,1:T(8,128)(2,1)}, bf16[256,2,1536]{2,0,1:T(8,128)(2,1)}, u32[]{:S(2)}, u32[]{:S(2)}) collective-permute-start(bf16[256,2,1536]{2,0,1:T(8,128)(2,1)} %slice_bitcast_fusion.7), channel_id=1, source_target_pairs={{0,32},{32,64},{64,96},{96,0},{1,33},{33,65},{65,97},{97,1},{2,34}... | collective-permute-start | bytes 4718600 | tf_op jit(solution)/shard_map/ppermute | solution.py:111
  311.6 94.7 %all-to-all-start.3 = ((bf16[32,2,16,2048]{3,2,1,0:T(8,128)(2,1)}), bf16[32,2,16,2048]{3,2,1,0:T(8,128)(2,1)}, u32[]{:S(2)}, u32[]{:S(2)}) async-start(bf16[32,2,16,2048]{3,2,1,0:T(8,128)(2,1)} %copy.118), calls=%async_computation.3 | async-start | bytes 8388608 | tf_op jit(solution)/shard_map/all_to_all | solution.py:54
  316.5 1.9 copy-start.8
  316.5 2.8 copy-start.3
  319.3 1.9 copy-start.2
  322.8 29.7 %collective-permute-start.7 = (bf16[384,2,512]{2,0,1:T(8,128)(2,1)S(1)}, bf16[384,2,512]{2,0,1:T(8,128)(2,1)S(1)}, u32[]{:S(2)}, u32[]{:S(2)}) collective-permute-start(bf16[384,2,512]{2,0,1:T(8,128)(2,1)S(1)} %fusion.40), channel_id=1, source_target_pairs={{0,32},{32,64},{64,96},{96,0},{1,33},{33,65},{65,97},{97,1},{2,34}... | collective-permute-start | bytes 2359304 | tf_op jit(solution)/shard_map/ppermute | solution.py:114
  324.2 28.5 %collective-permute-start.10 = (bf16[384,2,512]{2,0,1:T(8,128)(2,1)S(1)}, bf16[384,2,512]{2,0,1:T(8,128)(2,1)S(1)}, u32[]{:S(2)}, u32[]{:S(2)}) collective-permute-start(bf16[384,2,512]{2,0,1:T(8,128)(2,1)S(1)} %fusion.37), channel_id=1, source_target_pairs={{0,96},{32,0},{64,32},{96,64},{1,97},{33,1},{65,33},{97,65},{2,98}... | collective-permute-start | bytes 2359304 | tf_op jit(solution)/shard_map/ppermute | solution.py:115
  337.5 5.2 %copy-start.7 = (bf16[2,1,512,2,384]{2,4,3,1,0:T(8,128)(2,1)S(1)}, bf16[2,1,512,2,384]{2,4,3,1,0:T(8,128)(2,1)}, u32[]{:S(2)}) copy-start(bf16[2,1,512,2,384]{2,4,3,1,0:T(8,128)(2,1)} %get-tuple-element.27) | copy-start | bytes 4718596
  337.5 48.6 %collective-permute-start.1 = (bf16[256,2,1536]{2,0,1:T(8,128)(2,1)S(1)}, bf16[256,2,1536]{2,0,1:T(8,128)(2,1)S(1)}, u32[]{:S(2)}, u32[]{:S(2)}) collective-permute-start(bf16[256,2,1536]{2,0,1:T(8,128)(2,1)S(1)} %fusion.25), channel_id=1, source_target_pairs={{0,32},{32,64},{64,96},{96,0},{1,33},{33,65},{65,97},{97,1},{2,34}... | collective-permute-start | bytes 4718600 | tf_op jit(solution)/shard_map/ppermute | solution.py:114
  339.5 48.2 %collective-permute-start.4 = (bf16[256,2,1536]{2,0,1:T(8,128)(2,1)S(1)}, bf16[256,2,1536]{2,0,1:T(8,128)(2,1)S(1)}, u32[]{:S(2)}, u32[]{:S(2)}) collective-permute-start(bf16[256,2,1536]{2,0,1:T(8,128)(2,1)S(1)} %fusion.22), channel_id=1, source_target_pairs={{0,96},{32,0},{64,32},{96,64},{1,97},{33,1},{65,33},{97,65},{2,98}... | collective-permute-start | bytes 4718600 | tf_op jit(solution)/shard_map/ppermute | solution.py:115
  342.8 10.0 %copy-start.11 = (bf16[1,2,384,2,512]{4,2,1,0,3:T(8,128)(2,1)S(1)}, bf16[1,2,384,2,512]{4,2,1,0,3:T(8,128)(2,1)}, u32[]{:S(2)}) copy-start(bf16[1,2,384,2,512]{4,2,1,0,3:T(8,128)(2,1)} %get-tuple-element.32) | copy-start | bytes 4718596
  352.7 50.3 %collective-permute-start.8 = (bf16[384,2,512]{2,0,1:T(8,128)(2,1)S(1)}, bf16[384,2,512]{2,0,1:T(8,128)(2,1)S(1)}, u32[]{:S(2)}, u32[]{:S(2)}) collective-permute-start(bf16[384,2,512]{2,0,1:T(8,128)(2,1)S(1)} %fusion.39), channel_id=1, source_target_pairs={{0,32},{32,64},{64,96},{96,0},{1,33},{33,65},{65,97},{97,1},{2,34}... | collective-permute-start | bytes 2359304 | tf_op jit(solution)/shard_map/ppermute | solution.py:114
  352.8 34.9 %copy-start.5 = (bf16[1,2,256,2,1536]{4,2,1,0,3:T(8,128)(2,1)S(1)}, bf16[1,2,256,2,1536]{4,2,1,0,3:T(8,128)(2,1)}, u32[]{:S(2)}) copy-start(bf16[1,2,256,2,1536]{4,2,1,0,3:T(8,128)(2,1)} %get-tuple-element.23) | copy-start | bytes 9437188
  353.0 50.0 %collective-permute-start.11 = (bf16[384,2,512]{2,0,1:T(8,128)(2,1)S(1)}, bf16[384,2,512]{2,0,1:T(8,128)(2,1)S(1)}, u32[]{:S(2)}, u32[]{:S(2)}) collective-permute-start(bf16[384,2,512]{2,0,1:T(8,128)(2,1)S(1)} %fusion.36), channel_id=1, source_target_pairs={{0,96},{32,0},{64,32},{96,64},{1,97},{33,1},{65,33},{97,65},{2,98}... | collective-permute-start | bytes 2359304 | tf_op jit(solution)/shard_map/ppermute | solution.py:115
  387.7 5.0 %copy-start.6 = (bf16[2,1,512,2,384]{2,4,3,1,0:T(8,128)(2,1)S(1)}, bf16[2,1,512,2,384]{2,4,3,1,0:T(8,128)(2,1)}, u32[]{:S(2)}) copy-start(bf16[2,1,512,2,384]{2,4,3,1,0:T(8,128)(2,1)} %get-tuple-element.29) | copy-start | bytes 4718596
  387.7 46.9 %collective-permute-start.2 = (bf16[256,2,1536]{2,0,1:T(8,128)(2,1)}, bf16[256,2,1536]{2,0,1:T(8,128)(2,1)}, u32[]{:S(2)}, u32[]{:S(2)}) collective-permute-start(bf16[256,2,1536]{2,0,1:T(8,128)(2,1)} %fusion.24), channel_id=1, source_target_pairs={{0,32},{32,64},{64,96},{96,0},{1,33},{33,65},{65,97},{97,1},{2,34}... | collective-permute-start | bytes 4718600 | tf_op jit(solution)/shard_map/ppermute | solution.py:114
  387.7 5.1 %copy-start.1 = (bf16[2,1536,1,2,256]{1,4,3,2,0:T(8,128)(2,1)S(1)}, bf16[2,1536,1,2,256]{1,4,3,2,0:T(8,128)(2,1)}, u32[]{:S(2)}) copy-start(bf16[2,1536,1,2,256]{1,4,3,2,0:T(8,128)(2,1)} %get-tuple-element.20) | copy-start | bytes 9437188
  389.3 45.3 %collective-permute-start.5 = (bf16[256,2,1536]{2,0,1:T(8,128)(2,1)}, bf16[256,2,1536]{2,0,1:T(8,128)(2,1)}, u32[]{:S(2)}, u32[]{:S(2)}) collective-permute-start(bf16[256,2,1536]{2,0,1:T(8,128)(2,1)} %fusion.21), channel_id=1, source_target_pairs={{0,96},{32,0},{64,32},{96,64},{1,97},{33,1},{65,33},{97,65},{2,98}... | collective-permute-start | bytes 4718600 | tf_op jit(solution)/shard_map/ppermute | solution.py:115

commit v4 on v2

v4 whole, which is shorter than its diff:
```python
import jax
import jax.numpy as jnp
from jax import lax
from jax.experimental.layout import Layout, with_layout_constraint
from jax.sharding import PartitionSpec as P


def swiglu_forward(preact, hidden):
    gate_part = preact[..., :hidden]
    up_part = preact[..., hidden:]
    return gate_part * jax.nn.sigmoid(gate_part) * up_part


def swiglu_backward(preact, upstream, hidden):
    gate_part = preact[..., :hidden]
    up_part = preact[..., hidden:]
    sigmoid_value = jax.nn.sigmoid(gate_part)
    silu_value = gate_part * sigmoid_value
    derivative = sigmoid_value * (1.0 + gate_part * (1.0 - sigmoid_value))
    return jnp.concatenate([upstream * up_part * derivative, upstream * silu_value], axis=-1)


def per_device(tokens, target, expert_ids, gates, w_in, w_out):
    tok_rows, model_width = tokens.shape
    route_count = expert_ids.shape[1]
    hidden = w_out.shape[0]
    local_experts = w_in.shape[1]
    expert_peers = lax.axis_size("expert")
    experts_all = local_experts * expert_peers
    capacity = 3 * tok_rows * route_count // (2 * experts_all)
    slots_per = -(-capacity // 16) * 16
    slot_total = experts_all * slots_per
    routes = tok_rows * route_count
    flat_ids = expert_ids.T.reshape(routes)
    matches = (flat_ids[:, None] == jnp.arange(experts_all, dtype=jnp.int32)[None, :]).astype(
        jnp.int32
    )
    ranking = jnp.sum((jnp.cumsum(matches, axis=0) - 1) * matches, axis=1)
    slot_index = (
        (flat_ids % local_experts) * (expert_peers * slots_per)
        + (flat_ids // local_experts) * slots_per
        + ranking
    )
    route_onehot = (slot_index[:, None] == jnp.arange(slot_total, dtype=jnp.int32)[None, :]).astype(
        jnp.bfloat16
    )
    token_onehot = jnp.sum(
        route_onehot.reshape(route_count, tok_rows, slot_total).astype(jnp.float32), axis=0
    ).astype(jnp.bfloat16)
    gate_rows = gates.T
    block = expert_peers * slots_per

    def to_slots(onehot, rows):
        buffer = lax.dot_general(
            onehot, rows, (((0,), (0,)), ((), ())), preferred_element_type=jnp.float32
        ).astype(jnp.bfloat16)
        return buffer.reshape(local_experts, expert_peers, slots_per, model_width)

    def exchange(buffer):
        moved = lax.all_to_all(buffer, "expert", split_axis=0, concat_axis=0, tiled=True)
        return moved.reshape(block, buffer.shape[-1])

    def back(rows):
        return exchange(rows.reshape(expert_peers, slots_per, rows.shape[-1]))

    def mm(left, right, contract):
        return lax.dot_general(
            left, right, ((contract[0], contract[1]), ((), ())), preferred_element_type=jnp.float32
        )

    dispatched = to_slots(token_onehot, tokens)
    sent_rows, preact, activation, returned = [], [], [], []
    for e in range(local_experts):
        rows_e = exchange(dispatched[e])
        preact_e = mm(rows_e, w_in[:, e, :], ((1,), (0,)))
        activation_e = swiglu_forward(preact_e, hidden).astype(jnp.bfloat16)
        output_e = mm(activation_e, w_out[:, e, :], ((1,), (0,))).astype(jnp.bfloat16)
        returned.append(back(output_e))
        sent_rows.append(rows_e)
        preact.append(preact_e)
        activation.append(activation_e)
    returned = jnp.concatenate(returned, axis=0)
    route_rows = jnp.dot(route_onehot, returned, preferred_element_type=jnp.float32)
    student = tokens.astype(jnp.float32) + jnp.sum(
        route_rows.reshape(route_count, tok_rows, model_width) * gate_rows[:, :, None], axis=0
    )
    residual_grad = student - target.astype(jnp.float32)
    scaled = (gate_rows[:, :, None] * residual_grad[None, :, :]).astype(jnp.bfloat16)
    grads_dispatched = to_slots(route_onehot, scaled.reshape(routes, model_width))
    returned_grads, terms_in, terms_out = [], [], []
    for e in range(local_experts):
        grads_e = exchange(grads_dispatched[e])
        term_out_e = mm(activation[e], grads_e, ((0,), (0,))).astype(jnp.bfloat16)
        terms_out.append(lax.psum_scatter(term_out_e, "dp", scatter_dimension=1, tiled=True))
        act_grad_e = mm(grads_e, w_out[:, e, :], ((1,), (1,)))
        pre_grad_e = swiglu_backward(preact[e], act_grad_e, hidden).astype(jnp.bfloat16)
        input_grad_e = mm(pre_grad_e, w_in[:, e, :], ((1,), (1,))).astype(jnp.bfloat16)
        returned_grads.append(back(input_grad_e))
        term_in_e = mm(sent_rows[e], pre_grad_e, ((0,), (0,))).astype(jnp.bfloat16)
        terms_in.append(lax.psum_scatter(term_in_e, "dp", scatter_dimension=0, tiled=True))
    returned_grads = jnp.concatenate(returned_grads, axis=0)
    grad_tokens = (
        residual_grad + jnp.dot(token_onehot, returned_grads, preferred_element_type=jnp.float32)
    ).astype(jnp.bfloat16)
    row_major = Layout(major_to_minor=(0, 1, 2))
    grad_in = with_layout_constraint(jnp.stack(terms_in, axis=1), row_major)
    grad_out = with_layout_constraint(jnp.stack(terms_out, axis=1), row_major)
    return (grad_tokens, grad_in, grad_out)


def solution(mesh):
    in_specs = (
        P(("dp", "expert"), None),
        P(("dp", "expert"), None),
        P(("dp", "expert"), None),
        P(("dp", "expert"), None),
        P(None, "expert", None),
        P(None, "expert", None),
    )
    out_specs = (P(("dp", "expert"), None), P("dp", "expert", None), P(None, "expert", "dp"))
    return jax.shard_map(
        per_device, mesh=mesh, in_specs=in_specs, out_specs=out_specs, check_vma=False
    )
```

time: 431 us -> 442 us (1.026); the launches traced: 430 us -> 434 us
  blocking collectives: 171 us -> 97.3 us
  local copies, waits for them, and re-layouts: 22.4 us -> 73.1 us
  starting transfers between devices: 5.04 us -> 28.3 us
  waiting for transfers between devices: 137 us -> 120 us
  other arithmetic: 4.3 us -> 17.2 us
  matrix products: 75.9 us -> 82.8 us
    all_to_all x3, blocking collectives: 171 us -> 97.3 us  [exchange(): lax.all_to_all(buffer, 'expert', split_axis=0, concat_axis=0, tiled=True)]
    slice x1 -> x5, local copies, waits for them, and re-layouts: 0.27 us -> 43.3 us  [the longest x1 25.3 us: per_device(): preact_e = mm(rows_e, w_in[:, e, :], ((1,), (0,)))]
    reduce_scatter x2 -> x4, waiting for transfers between devices: 85 us -> 53.3 us  [the longest x2 53.2 us: per_device(): lax.psum_scatter(term_in_e, 'dp', scatter_dimension=0, tiled=True)]
    all_to_all x1 -> x5, starting transfers between devices: 4.78 us -> 27.9 us  [exchange(): lax.all_to_all(buffer, 'expert', split_axis=0, concat_axis=0, tiled=True)]
    all_to_all x1 -> x5, waiting for transfers between devices: 51.9 us -> 67.1 us  [exchange(): lax.all_to_all(buffer, 'expert', split_axis=0, concat_axis=0, tiled=True)]
    another operation x2 -> x4, other arithmetic: 1.52 us -> 14 us  [the longest x1 8.05 us: per_device(): grad_in = with_layout_constraint(jnp.stack(terms_in, axis=1), row_major)]
    another operation x0 -> x4, local copies, waits for them, and re-layouts: none -> 12.4 us  [the longest x2 7.67 us: per_device(): grad_in = with_layout_constraint(jnp.stack(terms_in, axis=1), row_major)]
    dot_general x6 -> x12, matrix products: 61.9 us -> 70.3 us  [mm(): lax.dot_general(left, right, ((contract[0], contract[1]), ((), ())), pref...]
  transfers between devices with their start and end apart: 3 -> 9, of which waited for: 2 -> 6; matrix products, arithmetic and copies ran while one was open for 9% -> 28% of each run, Pallas kernels for 0% -> 0%
where the time goes in v4:
time: 442 us; the launch traced here: 434 us
  waiting for transfers between devices  120 us (27%)
  blocking collectives  97.3 us (22%)
  matrix products  82.8 us (19%)
  local copies, waits for them, and re-layouts  73.1 us (17%)
  starting transfers between devices  28.3 us (6%)
  other arithmetic  17.2 us (4%)
  between operations  14.6 us (3%)
    all_to_all x3, blocking collectives, exchange(): lax.all_to_all(buffer, 'expert', split_axis=0, concat_axis=0, tiled=True)  97.3 us
    dot_general x12, matrix products, mm(): lax.dot_general(left, right, ((contract[0], contract[1]), ((), ())), pref...  70.3 us
    all_to_all x5, waiting for transfers between devices, exchange(): lax.all_to_all(buffer, 'expert', split_axis=0, concat_axis=0, tiled=True)  67.1 us
    reduce_scatter x2, waiting for transfers between devices, per_device(): lax.psum_scatter(term_in_e, 'dp', scatter_dimension=0, tiled=True)  53.2 us
    all_to_all x5, starting transfers between devices, exchange(): lax.all_to_all(buffer, 'expert', split_axis=0, concat_axis=0, tiled=True)  27.9 us
    slice x1, local copies, waits for them, and re-layouts, per_device(): preact_e = mm(rows_e, w_in[:, e, :], ((1,), (0,)))  25.3 us
    unnamed x56, local copies, waits for them, and re-layouts  15.7 us
    slice x1, local copies, waits for them, and re-layouts, per_device(): w_out[:, e, :]  14.7 us
  transfers between devices with their start and end apart: 9, of which 6 were waited for; matrix products, arithmetic and copies ran while one was open for 28% of the time, Pallas kernels for 0%

profile of v4, /device:TPU:1, one launch (start us, length us, event | category | flops | bytes accessed | tf_op | source)
XLA Modules:
  0.0 433.7 jit_solution(10444533490921117799)
XLA Ops:
  8.7 1.5 reduce-window.6
  12.6 2.4 convolution_convert_fusion.3
  15.0 2.5 fusion.51
  17.5 8.6 %all-to-all-start = ((bf16[32,16,2048]{2,1,0:T(8,128)(2,1)}), bf16[32,16,2048]{2,1,0:T(8,128)(2,1)S(1)}, u32[]{:S(2)}, u32[]{:S(2)}) async-start(bf16[32,16,2048]{2,1,0:T(8,128)(2,1)} %bitcast.2), calls=%async_computation | async-start | bytes 4194304 | tf_op jit(solution)/shard_map/all_to_all | solution.py:60
  26.1 25.3 %fusion.48 = (bf16[2048,1,1536]{2,1,0:T(2,128)(2,1)}, bf16[2048,1,1536]{2,1,0:T(2,128)(2,1)}) fusion(bf16[2048,2,1536]{2,1,0:T(2,128)(2,1)} %param.10), kind=kLoop, calls=%fused_computation.92 | loop fusion | bytes 25165824 | tf_op jit(solution)/shard_map/slice | solution.py:75
  51.4 3.0 all-to-all-done
  54.4 1.3 copy-done.9
  55.7 4.5 %all-to-all-start.2 = ((bf16[32,16,2048]{2,1,0:T(8,128)(2,1)}), bf16[32,16,2048]{2,1,0:T(8,128)(2,1)S(1)}, u32[]{:S(2)}, u32[]{:S(2)}) async-start(bf16[32,16,2048]{2,1,0:T(8,128)(2,1)} %bitcast.8), calls=%async_computation.2 | async-start | bytes 4194304 | tf_op jit(solution)/shard_map/all_to_all | solution.py:60
  60.2 14.7 %fusion.49 = (bf16[768,1,2048]{2,1,0:T(2,128)(2,1)S(1)}, bf16[768,1,2048]{2,1,0:T(2,128)(2,1)}) fusion(bf16[768,2,2048]{2,1,0:T(2,128)(2,1)} %param.11), kind=kLoop, calls=%fused_computation.93 | loop fusion | bytes 12582912 | tf_op jit(solution)/shard_map/slice | solution.py:77
  75.0 3.4 fusion.16
  78.4 1.8 copy-done.3
  80.7 0.9 copy-done.14
  81.6 3.6 convolution_convert_fusion.9
  85.2 3.4 all-to-all-done.2
  88.6 1.3 copy-done.7
  89.9 6.0 %all-to-all-start.1 = ((bf16[32,16,2048]{2,1,0:T(8,128)(2,1)}), bf16[32,16,2048]{2,1,0:T(8,128)(2,1)}, u32[]{:S(2)}, u32[]{:S(2)}) async-start(bf16[32,16,2048]{2,1,0:T(8,128)(2,1)} %bitcast.96), calls=%async_computation.1 | async-start | bytes 4194304 | tf_op jit(solution)/shard_map/all_to_all | solution.py:60
  95.9 7.4 %fusion.17 = f32[512,1536]{1,0:T(8,128)S(1)} fusion(bf16[512,2048]{1,0:T(8,128)(2,1)} %bitcast.85, bf16[2048,1,1536]{2,1,0:T(2,128)(2,1)} %get-tuple-element.4), kind=kOutput, calls=%fused_computation.32 | convolution fusion | flops 3221225472 | bytes 11534336 | tf_op jit(solution)/shard_map/dot_general | solution.py:67
  103.4 1.7 copy-done.2
  106.4 3.6 convolution_convert_fusion.8
  110.0 14.1 %all-to-all-done.1 = bf16[32,16,2048]{2,1,0:T(8,128)(2,1)} async-done(((bf16[32,16,2048]{2,1,0:T(8,128)(2,1)}), bf16[32,16,2048]{2,1,0:T(8,128)(2,1)}, u32[]{:S(2)}, u32[]{:S(2)}) %all-to-all-start.1) | async-done | bytes 2097184 | tf_op jit(solution)/shard_map/all_to_all | solution.py:60
  124.1 4.7 %all-to-all-start.3 = ((bf16[32,16,2048]{2,1,0:T(8,128)(2,1)}), bf16[32,16,2048]{2,1,0:T(8,128)(2,1)S(1)}, u32[]{:S(2)}, u32[]{:S(2)}) async-start(bf16[32,16,2048]{2,1,0:T(8,128)(2,1)} %bitcast.95), calls=%async_computation.3 | async-start | bytes 4194304 | tf_op jit(solution)/shard_map/all_to_all | solution.py:60
  129.0 28.2 %all-to-all-done.3 = bf16[32,16,2048]{2,1,0:T(8,128)(2,1)S(1)} async-done(((bf16[32,16,2048]{2,1,0:T(8,128)(2,1)}), bf16[32,16,2048]{2,1,0:T(8,128)(2,1)S(1)}, u32[]{:S(2)}, u32[]{:S(2)}) %all-to-all-start.3) | async-done | bytes 2097184 | tf_op jit(solution)/shard_map/all_to_all | solution.py:60
  157.2 4.5 %fusion.1 = f32[640,2048]{1,0:T(8,128)S(1)} fusion(bf16[512,2048]{1,0:T(8,128)(2,1)S(1)} %bitcast.94, bf16[512,2048]{1,0:T(8,128)(2,1)} %bitcast.7, s32[640]{0:T(1024)S(1)} %fusion.30), kind=kOutput, calls=%fused_computation.7 | convolution fusion | flops 2693398528 | bytes 9439744 | tf_op jit(solution)/shard_map/dot_general | solution.py:83
  163.6 4.0 convolution_convert_fusion.2
  168.0 32.1 %all_to_all.40 = bf16[32,16,2048]{2,1,0:T(8,128)(2,1)S(1)} all-to-all(bf16[32,16,2048]{2,1,0:T(8,128)(2,1)S(1)} %bitcast.81), channel_id=1, replica_groups=mesh['dp'=4,'expert'=32] {'expert'}, dimensions={0} | all-to-all | bytes 4194304 | tf_op jit(solution)/shard_map/all_to_all | solution.py:60
  200.1 1.3 copy-done.12
  201.4 3.5 convolution_convert_fusion.4
  204.9 32.0 %all_to_all.41 = bf16[32,16,2048]{2,1,0:T(8,128)(2,1)S(1)} all-to-all(bf16[32,16,2048]{2,1,0:T(8,128)(2,1)S(1)} %bitcast.80), channel_id=1, replica_groups=mesh['dp'=4,'expert'=32] {'expert'}, dimensions={0} | all-to-all | bytes 4194304 | tf_op jit(solution)/shard_map/all_to_all | solution.py:60
  236.9 1.3 copy-done.13
  238.3 3.5 convolution_convert_fusion.5
  241.9 7.3 %multiply_convert_fusion.3 = (bf16[512,768]{1,0:T(8,128)(2,1)S(1)}, bf16[512,768]{1,0:T(8,128)(2,1)S(1)}) fusion(f32[512,1536]{1,0:T(8,128)} %copy-done.3, bf16[512,2048]{1,0:T(8,128)(2,1)} %bitcast.92, bf16[768,1,2048]{2,1,0:T(2,128)(2,1)} %copy-done.1), kind=kOutput, calls=%fused_computation.39 | convolution fusion | flops 1615724544 | bytes 9961472 | tf_op jit(solution)/shard_map/dot_general | solution.py:67
  250.4 5.8 %convolution_convert_fusion.1 = bf16[2048,1536]{1,0:T(8,128)(2,1)} fusion(bf16[512,2048]{1,0:T(8,128)(2,1)S(1)} %bitcast.88, bf16[512,768]{1,0:T(8,128)(2,1)S(1)} %get-tuple-element.8, bf16[512,768]{1,0:T(8,128)(2,1)S(1)} %get-tuple-element.7), kind=kOutput, calls=%fused_computation.1 | convolution fusion | flops 3227516928 | bytes 9961472 | tf_op jit(solution)/shard_map/dot_general | solution.py:67
  256.5 7.4 %multiply_convert_fusion.1 = (bf16[512,768]{1,0:T(8,128)(2,1)S(1)}, bf16[512,768]{1,0:T(8,128)(2,1)S(1)}) fusion(f32[512,1536]{1,0:T(8,128)} %copy-done.2, bf16[512,2048]{1,0:T(8,128)(2,1)} %bitcast.90, bf16[768,1,2048]{2,1,0:T(2,128)(2,1)} %get-tuple-element.6), kind=kOutput, calls=%fused_computation.37 | convolution fusion | flops 1615724544 | bytes 9961472 | tf_op jit(solution)/shard_map/dot_general | solution.py:67
  265.1 5.6 %convolution_convert_fusion = bf16[2048,1536]{1,0:T(8,128)(2,1)} fusion(bf16[512,2048]{1,0:T(8,128)(2,1)S(1)} %bitcast.86, bf16[512,768]{1,0:T(8,128)(2,1)S(1)} %get-tuple-element.10, bf16[512,768]{1,0:T(8,128)(2,1)S(1)} %get-tuple-element.9), kind=kOutput, calls=%fused_computation | convolution fusion | flops 3227516928 | bytes 9961472 | tf_op jit(solution)/shard_map/dot_general | solution.py:67
  270.7 1.1 copy-done.23
  272.0 9.3 %convolution_convert_fusion.6 = bf16[512,2048]{1,0:T(8,128)(2,1)} fusion(bf16[2048,1,1536]{2,1,0:T(2,128)(2,1)} %get-tuple-element.4, bf16[512,768]{1,0:T(8,128)(2,1)S(1)} %copy-done.25, bf16[512,768]{1,0:T(8,128)(2,1)S(1)} %copy-done.23), kind=kOutput, calls=%fused_computation.22 | convolution fusion | flops 3225419776 | bytes 9961472 | tf_op jit(solution)/shard_map/dot_general | solution.py:67
  281.3 4.2 all-to-all-start.7
  285.5 9.8 %convolution_convert_fusion.7 = bf16[512,2048]{1,0:T(8,128)(2,1)} fusion(bf16[2048,1,1536]{2,1,0:T(2,128)(2,1)} %get-tuple-element.3, bf16[512,768]{1,0:T(8,128)(2,1)} %copy-done.21, bf16[512,768]{1,0:T(8,128)(2,1)} %copy-done.20), kind=kOutput, calls=%fused_computation.23 | convolution fusion | flops 3225419776 | bytes 9961472 | tf_op jit(solution)/shard_map/dot_general | solution.py:67
  295.3 18.5 %all-to-all-done.7 = bf16[32,16,2048]{2,1,0:T(8,128)(2,1)S(1)} async-done(((bf16[32,16,2048]{2,1,0:T(8,128)(2,1)}), bf16[32,16,2048]{2,1,0:T(8,128)(2,1)S(1)}, u32[]{:S(2)}, u32[]{:S(2)}) %all-to-all-start.7) | async-done | bytes 2097184 | tf_op jit(solution)/shard_map/all_to_all | solution.py:60
  313.8 33.2 %all_to_all.42 = bf16[32,16,2048]{2,1,0:T(8,128)(2,1)S(1)} all-to-all(bf16[32,16,2048]{2,1,0:T(8,128)(2,1)} %bitcast.98), channel_id=1, replica_groups=mesh['dp'=4,'expert'=32] {'expert'}, dimensions={0} | all-to-all | bytes 4194304 | tf_op jit(solution)/shard_map/all_to_all | solution.py:60
  346.9 1.7 fusion.13
  348.6 2.4 copy.26
  351.0 2.3 copy.25
  353.4 4.4 %pad_maximum_fusion.3 = bf16[768,2,512]{2,1,0:T(2,128)(2,1)} fusion(bf16[768,1,512]{2,1,0:T(2,128)(2,1)S(1)} %copy.26, bf16[768,1,512]{2,1,0:T(2,128)(2,1)S(1)} %copy.25), kind=kLoop, calls=%fused_computation.35 | loop fusion | flops 3145728 | bytes 3145728 | tf_op jit(solution)/shard_map/stack | solution.py:107
  357.8 3.8 copy.23
  361.6 53.2 %reduce-scatter.7.cloned.1.call-done = bf16[512,1536]{1,0:T(8,128)(2,1)} async-done(((bf16[2048,1536]{1,0:T(8,128)(2,1)}), bf16[512,1536]{1,0:T(8,128)(2,1)}) %reduce-scatter.7.cloned.1.call-update) | async-done | bytes 1572880 | tf_op jit(solution)/shard_map/reduce_scatter | solution.py:100
  414.9 3.8 copy.24
  418.7 8.0 %pad_maximum_fusion = bf16[512,2,1536]{2,1,0:T(2,128)(2,1)} fusion(bf16[512,1,1536]{2,1,0:T(2,128)(2,1)S(1)} %copy.24, bf16[512,1,1536]{2,1,0:T(2,128)(2,1)S(1)} %copy.23), kind=kLoop, calls=%fused_computation.19 | loop fusion | flops 6291456 | bytes 6291456 | tf_op jit(solution)/shard_map/stack | solution.py:106
  (77 shorter events, 11.2 us)
Async XLA Ops:
  11.8 0.7 copy-start.5
  17.5 36.9 %all-to-all-start = ((bf16[32,16,2048]{2,1,0:T(8,128)(2,1)}), bf16[32,16,2048]{2,1,0:T(8,128)(2,1)S(1)}, u32[]{:S(2)}, u32[]{:S(2)}) async-start(bf16[32,16,2048]{2,1,0:T(8,128)(2,1)} %bitcast.2), calls=%async_computation | async-start | bytes 4194304 | tf_op jit(solution)/shard_map/all_to_all | solution.py:60
  54.4 1.3 copy-start.9
  55.7 32.9 %all-to-all-start.2 = ((bf16[32,16,2048]{2,1,0:T(8,128)(2,1)}), bf16[32,16,2048]{2,1,0:T(8,128)(2,1)S(1)}, u32[]{:S(2)}, u32[]{:S(2)}) async-start(bf16[32,16,2048]{2,1,0:T(8,128)(2,1)} %bitcast.8), calls=%async_computation.2 | async-start | bytes 4194304 | tf_op jit(solution)/shard_map/all_to_all | solution.py:60
  60.2 14.8 %copy-start = (bf16[2048,1,1536]{2,1,0:T(2,128)(2,1)S(1)}, bf16[2048,1,1536]{2,1,0:T(2,128)(2,1)}, u32[]{:S(2)}) copy-start(bf16[2048,1,1536]{2,1,0:T(2,128)(2,1)} %get-tuple-element.3) | copy-start | bytes 18874372
  60.2 14.8 %copy-start.10 = (bf16[32,16,2048]{2,1,0:T(8,128)(2,1)S(1)}, bf16[32,16,2048]{2,1,0:T(8,128)(2,1)}, u32[]{:S(2)}) copy-start(bf16[32,16,2048]{2,1,0:T(8,128)(2,1)} %copy-done.9) | copy-start | bytes 6291460
  75.0 5.7 %copy-start.1 = (bf16[768,1,2048]{2,1,0:T(2,128)(2,1)}, bf16[768,1,2048]{2,1,0:T(2,128)(2,1)S(1)}, u32[]{:S(2)}) copy-start(bf16[768,1,2048]{2,1,0:T(2,128)(2,1)S(1)} %get-tuple-element.5) | copy-start | bytes 9437188
  78.4 1.8 copy-start.3
  80.7 0.9 copy-start.14
  88.6 1.3 copy-start.7
  89.9 16.5 %slice-start = ((s8[6291456]{0:T(1024)(128)(4,1)}), s8[2097152]{0:T(1024)(128)(4,1)S(1)}, s32[]{:S(2)}) async-start(s8[6291456]{0:T(1024)(128)(4,1)} %bitcast.82), calls=%async_computation.16 | async-start | bytes 4194304
  89.9 34.2 %all-to-all-start.1 = ((bf16[32,16,2048]{2,1,0:T(8,128)(2,1)}), bf16[32,16,2048]{2,1,0:T(8,128)(2,1)}, u32[]{:S(2)}, u32[]{:S(2)}) async-start(bf16[32,16,2048]{2,1,0:T(8,128)(2,1)} %bitcast.96), calls=%async_computation.1 | async-start | bytes 4194304 | tf_op jit(solution)/shard_map/all_to_all | solution.py:60
  95.9 10.5 %slice-start.1 = ((s8[6291456]{0:T(1024)(128)(4,1)}), s8[4194304]{0:T(1024)(128)(4,1)S(1)}, s32[]{:S(2)}) async-start(s8[6291456]{0:T(1024)(128)(4,1)} %bitcast.82), calls=%async_computation.17 | async-start | bytes 8388608
  103.3 1.7 copy-start.2
  105.5 0.9 copy-start.16
  124.1 4.7 %copy-start.19 = (f32[160,4]{0,1:T(4,128)S(1)}, f32[160,4]{0,1:T(4,128)}, u32[]{:S(2)}) copy-start(f32[160,4]{0,1:T(4,128)} %param.9) | copy-start | bytes 7684
  124.1 33.0 %all-to-all-start.3 = ((bf16[32,16,2048]{2,1,0:T(8,128)(2,1)}), bf16[32,16,2048]{2,1,0:T(8,128)(2,1)S(1)}, u32[]{:S(2)}, u32[]{:S(2)}) async-start(bf16[32,16,2048]{2,1,0:T(8,128)(2,1)} %bitcast.95), calls=%async_computation.3 | async-start | bytes 4194304 | tf_op jit(solution)/shard_map/all_to_all | solution.py:60
  128.8 219.8 %reduce-scatter.11.cloned.1.call-start = ((), (), s32[]{:S(2)}) async-start(), calls=%async_computation.15 | async-start | bytes 3932160 | tf_op jit(solution)/shard_map/reduce_scatter | solution.py:94
  161.7 1.1 copy-start.4
  161.7 1.3 copy-start.18
  168.0 33.4 %copy-start.17 = (bf16[512,768]{1,0:T(8,128)(2,1)S(1)}, bf16[512,768]{1,0:T(8,128)(2,1)}, u32[]{:S(2)}) copy-start(bf16[512,768]{1,0:T(8,128)(2,1)} %copy-done.16) | copy-start | bytes 2359300
  200.1 1.3 copy-start.12
  204.9 146.1 %reduce-scatter.9.cloned.1.call-start = ((), (), s32[]{:S(2)}) async-start(), calls=%async_computation.14 | async-start | bytes 3932160 | tf_op jit(solution)/shard_map/reduce_scatter | solution.py:94
  204.9 33.3 %copy-start.15 = (bf16[512,768]{1,0:T(8,128)(2,1)S(1)}, bf16[512,768]{1,0:T(8,128)(2,1)}, u32[]{:S(2)}) copy-start(bf16[512,768]{1,0:T(8,128)(2,1)} %copy-done.14) | copy-start | bytes 2359300
  236.9 1.3 copy-start.13
  241.8 8.6 %copy-start.11 = (bf16[32,16,2048]{2,1,0:T(8,128)(2,1)S(1)}, bf16[32,16,2048]{2,1,0:T(8,128)(2,1)}, u32[]{:S(2)}) copy-start(bf16[32,16,2048]{2,1,0:T(8,128)(2,1)} %copy-done.9) | copy-start | bytes 6291460
  241.8 116.0 %reduce-scatter.5.cloned.1.call-start = ((), (), s32[]{:S(2)}) async-start(), calls=%async_computation.12 | async-start | bytes 7864320 | tf_op jit(solution)/shard_map/reduce_scatter | solution.py:100
  249.2 0.9 copy-start.20
  249.2 1.2 copy-start.21
  256.3 8.8 %copy-start.8 = (bf16[32,16,2048]{2,1,0:T(8,128)(2,1)S(1)}, bf16[32,16,2048]{2,1,0:T(8,128)(2,1)}, u32[]{:S(2)}) copy-start(bf16[32,16,2048]{2,1,0:T(8,128)(2,1)} %copy-done.7) | copy-start | bytes 6291460
  256.3 158.6 %reduce-scatter.7.cloned.1.call-start = ((), (), s32[]{:S(2)}) async-start(), calls=%async_computation.13 | async-start | bytes 7864320 | tf_op jit(solution)/shard_map/reduce_scatter | solution.py:100
  263.9 0.9 copy-start.22
  264.0 1.1 copy-start.24
  270.6 1.1 copy-start.23
  270.7 1.4 copy-start.25
  281.3 32.5 %all-to-all-start.7 = ((bf16[32,16,2048]{2,1,0:T(8,128)(2,1)}), bf16[32,16,2048]{2,1,0:T(8,128)(2,1)S(1)}, u32[]{:S(2)}, u32[]{:S(2)}) async-start(bf16[32,16,2048]{2,1,0:T(8,128)(2,1)} %bitcast.97), calls=%async_computation.7 | async-start | bytes 4194304 | tf_op jit(solution)/shard_map/all_to_all | solution.py:60
  313.8 33.2 %copy-start.6 = (bf16[160,1024]{1,0:T(8,128)(2,1)S(1)}, bf16[160,1024]{1,0:T(8,128)(2,1)}, u32[]{:S(2)}) copy-start(bf16[160,1024]{1,0:T(8,128)(2,1)} %copy-done.5) | copy-start | bytes 983044
Sparse Core Ops, SparseCore 0:
  205.0 37.0 reduce-scatter.10
  244.5 38.0 reduce-scatter.8
  285.0 63.7 reduce-scatter.4
  351.1 63.7 reduce-scatter.6

commit v5 on v2

--- a/solution.py
+++ b/solution.py
@@ -84,11 +84,33 @@
         lax.psum_scatter(
             term_in.astype(jnp.bfloat16), "dp", scatter_dimension=0, tiled=True
         ).astype(jnp.float32),
-        lax.psum_scatter(
-            term_out.astype(jnp.bfloat16), "dp", scatter_dimension=2, tiled=True
-        ).astype(jnp.float32),
+        ring_reduce_scatter(term_out.astype(jnp.bfloat16)).astype(jnp.float32),
     )
     return (grad_tokens, grad_in.astype(jnp.bfloat16), grad_out.astype(jnp.bfloat16))
+
+
+def ring_reduce_scatter(partial):
+    if partial.shape[1] != 2:
+        return lax.psum_scatter(partial, "dp", scatter_dimension=2, tiled=True)
+    peers = lax.axis_size("dp")
+    me = lax.axis_index("dp")
+    width = partial.shape[2] // peers
+    forward = [(i, (i + 1) % peers) for i in range(peers)]
+    backward = [(i, (i - 1) % peers) for i in range(peers)]
+
+    def own(offset, direction):
+        index = lax.rem(me + offset + peers, peers)
+        return lax.dynamic_slice_in_dim(partial[:, direction, :], index * width, width, axis=1)
+
+    def add(left, right):
+        return (left.astype(jnp.float32) + right.astype(jnp.float32)).astype(jnp.bfloat16)
+
+    up = lax.ppermute(own(-1, 0), "dp", forward)
+    down = lax.ppermute(own(1, 1), "dp", backward)
+    for step in range(2, peers):
+        up = lax.ppermute(add(up, own(-step, 0)), "dp", forward)
+        down = lax.ppermute(add(down, own(step, 1)), "dp", backward)
+    return jnp.stack([add(up, own(0, 0)), add(down, own(0, 1))], axis=1)
 
 
 def solution(mesh):

time: 431 us -> 442 us (1.026); the launches traced: 430 us -> 436 us
  blocking collectives: 171 us -> 117 us
  waiting for transfers between devices: 137 us -> 153 us
  starting transfers between devices: 5.04 us -> 20.6 us
  matrix products: 75.9 us -> 90.3 us
  other arithmetic: 4.3 us -> 16.6 us
    ppermute x0 -> x6, waiting for transfers between devices: none -> 101 us  [the longest x2 63.4 us: ring_reduce_scatter(): down = lax.ppermute(add(down, own(step, 1)), 'dp', backward)]
    reduce_scatter x1, waiting for transfers between devices: 85 us -> 0.01 us  [per_device(): lax.psum_scatter(term_in.astype(jnp.bfloat16), 'dp', scatter_dimension=0,...]
    all_to_all x3 -> x2, blocking collectives: 171 us -> 117 us  [exchange(): lax.all_to_all(buffer, 'expert', split_axis=0, concat_axis=0, tiled=True)]
    ppermute x0 -> x6, starting transfers between devices: none -> 10.2 us  [the longest x2 6.98 us: ring_reduce_scatter(): down = lax.ppermute(add(down, own(step, 1)), 'dp', backward)]
    dot_general x1, matrix products: 11.3 us -> 21.4 us  [per_device(): jnp.einsum('sekh,deh->sekd', pre_grad, w_in, preferred_element_type=jnp.f...]
    convert_element_type x0 -> x4, other arithmetic: none -> 9.3 us  [add(): (left.astype(jnp.float32) + right.astype(jnp.float32)).astype(jnp.bfloat16)]
    all_to_all x1 -> x2, starting transfers between devices: 4.78 us -> 10.1 us  [exchange(): lax.all_to_all(buffer, 'expert', split_axis=0, concat_axis=0, tiled=True)]
    unnamed x24 -> x32, local copies, waits for them, and re-layouts: 17.4 us -> 15.2 us
  transfers between devices with their start and end apart: 3 -> 9, of which waited for: 2 -> 5; matrix products, arithmetic and copies ran while one was open for 9% -> 12% of each run, Pallas kernels for 0% -> 0%
where the time goes in v5:
time: 442 us; the launch traced here: 436 us
  waiting for transfers between devices  153 us (35%)
  blocking collectives  117 us (26%)
  matrix products  90.3 us (20%)
  local copies, waits for them, and re-layouts  24.4 us (6%)
  starting transfers between devices  20.6 us (5%)
  other arithmetic  16.6 us (4%)
  between operations  14.5 us (3%)
    all_to_all x2, blocking collectives, exchange(): lax.all_to_all(buffer, 'expert', split_axis=0, concat_axis=0, tiled=True)  117 us
    ppermute x2, waiting for transfers between devices, ring_reduce_scatter(): down = lax.ppermute(add(down, own(step, 1)), 'dp', backward)  63.4 us
    all_to_all x2, waiting for transfers between devices, exchange(): lax.all_to_all(buffer, 'expert', split_axis=0, concat_axis=0, tiled=True)  51.8 us
    ppermute x1, waiting for transfers between devices, ring_reduce_scatter(): down = lax.ppermute(own(1, 1), 'dp', backward)  33.5 us
    dot_general x1, matrix products, per_device(): jnp.einsum('sekh,deh->sekd', pre_grad, w_in, preferred_element_type=jnp.f...  21.4 us
    unnamed x32, local copies, waits for them, and re-layouts  15.2 us
    dot_general x1, matrix products, per_device(): jnp.einsum('sekd,deh->sekh', sent_rows, w_in, preferred_element_type=jnp....  12.4 us
    dot_general x1, matrix products, per_device(): jnp.einsum('sekd,sekh->deh', sent_rows, pre_grad, preferred_element_type=...  11.8 us
  transfers between devices with their start and end apart: 9, of which 5 were waited for; matrix products, arithmetic and copies ran while one was open for 12% of the time, Pallas kernels for 0%

profile of v5, /device:TPU:1, one launch (start us, length us, event | category | flops | bytes accessed | tf_op | source)
XLA Modules:
  0.0 435.8 jit_solution(8151098982252826589)
XLA Ops:
  7.2 0.8 eq.67
  7.9 0.8 eq.71
  8.7 1.5 reduce-window.6
  10.2 0.3 slice_reduce_fusion
  10.7 0.7 multiply_add_fusion.1
  11.4 0.4 fusion.36
  11.8 2.5 convolution_convert_fusion.1
  14.4 59.0 %all_to_all.20 = bf16[32,2,16,2048]{3,2,1,0:T(8,128)(2,1)S(1)} all-to-all(bf16[32,2,16,2048]{3,2,1,0:T(8,128)(2,1)S(1)} %bitcast.98), channel_id=1, replica_groups=mesh['dp'=4,'expert'=32] {'expert'}, dimensions={0} | all-to-all | bytes 8388608 | tf_op jit(solution)/shard_map/all_to_all | solution.py:54
  73.4 12.4 %fusion.11 = f32[32,2,16,1536]{3,2,0,1:T(8,128)S(1)} fusion(bf16[2048,2,1536,1]{2,1,0,3:T(2,128)(2,1)} %bitcast.107, bf16[32,2,16,2048]{3,2,1,0:T(8,128)(2,1)S(1)} %all_to_all.20), kind=kOutput, calls=%fused_computation.15 | convolution fusion | flops 6442450944 | bytes 23068672 | tf_op jit(solution)/shard_map/sekd,deh->sekh/dot_general | solution.py:57
  85.8 1.0 multiply_convert_fusion
  86.8 1.7 copy-done.3
  88.5 11.8 %convert_bitcast_fusion.1 = bf16[32,2,16,2048]{3,2,0,1:T(8,128)(2,1)S(1)} fusion(bf16[32,2,16,768]{3,2,0,1:T(8,128)(2,1)S(1)} %multiply_convert_fusion, bf16[768,2,2048,1]{2,1,0,3:T(2,128)(2,1)} %bitcast.109), kind=kOutput, calls=%fused_computation.18 | convolution fusion | flops 3223322624 | bytes 12058624 | tf_op jit(solution)/shard_map/sekh,hed->sekd/dot_general | solution.py:59
  100.3 2.5 copy.53
  102.8 4.8 %all-to-all-start.1 = ((bf16[32,2,16,2048]{3,2,1,0:T(8,128)(2,1)}), bf16[32,2,16,2048]{3,2,1,0:T(8,128)(2,1)}, u32[]{:S(2)}, u32[]{:S(2)}) async-start(bf16[32,2,16,2048]{3,2,1,0:T(8,128)(2,1)} %copy.53), calls=%async_computation.1 | async-start | bytes 8388608 | tf_op jit(solution)/shard_map/all_to_all | solution.py:54
  107.6 0.3 reduce-scatter.2.cloned.1.call-start
  108.0 51.8 %all-to-all-done.1 = bf16[32,2,16,2048]{3,2,1,0:T(8,128)(2,1)} async-done(((bf16[32,2,16,2048]{3,2,1,0:T(8,128)(2,1)}), bf16[32,2,16,2048]{3,2,1,0:T(8,128)(2,1)}, u32[]{:S(2)}, u32[]{:S(2)}) %all-to-all-start.1) | async-done | bytes 4194336 | tf_op jit(solution)/shard_map/all_to_all | solution.py:54
  159.8 5.7 %multiply_reduce_fusion = f32[160,2048]{1,0:T(8,128)S(1)} fusion(bf16[1024,2048,1]{1,0,2:T(8,128)(2,1)} %bitcast.9, f32[4,160]{1,0:T(4,128)S(1)} %bitcast.106, s32[4,160]{1,0:T(4,128)S(1)} %multiply_add_fusion.1), kind=kOutput, calls=%fused_computation.14 | convolution fusion | flops 2687303680 | bytes 5510144 | tf_op jit(solution)/shard_map/dot_general | solution.py:63
  165.6 0.2 convert_subtract_fusion
  165.8 0.3 fusion.10
  166.2 4.0 convolution_convert_fusion
  170.2 57.5 %all_to_all.21 = bf16[32,2,16,2048]{3,2,1,0:T(8,128)(2,1)S(1)} all-to-all(bf16[32,2,16,2048]{3,2,1,0:T(8,128)(2,1)S(1)} %bitcast.101), channel_id=1, replica_groups=mesh['dp'=4,'expert'=32] {'expert'}, dimensions={0} | all-to-all | bytes 8388608 | tf_op jit(solution)/shard_map/all_to_all | solution.py:54
  227.7 11.2 %fusion.22 = (bf16[32,2,16,768]{3,2,0,1:T(8,128)(2,1)S(1)}, bf16[32,2,16,768]{3,2,0,1:T(8,128)(2,1)}) fusion(f32[32,2,16,1536]{3,2,0,1:T(8,128)S(1)} %bitcast.100, bf16[768,2,2048,1]{2,1,0,3:T(2,128)(2,1)} %bitcast.110, bf16[32,2,16,2048]{3,2,1,0:T(8,128)(2,1)S(1)} %all_to_all.21), kind=kOutput, calls=%fused_computation.27 | convolution fusion | flops 3231449088 | bytes 19922944 | tf_op jit(solution)/shard_map/sekd,hed->sekh/dot_general | solution.py:70
  238.9 11.8 %fusion.4 = bf16[2048,2,1536]{0,2,1:T(8,128)(2,1)} fusion(bf16[32,2,16,2048]{3,2,1,0:T(8,128)(2,1)} %copy-done.7, bf16[32,2,16,768]{3,2,0,1:T(8,128)(2,1)} %get-tuple-element.16, bf16[32,2,16,768]{3,2,0,1:T(8,128)(2,1)S(1)} %get-tuple-element.15), kind=kOutput, calls=%fused_computation.6 | convolution fusion | flops 6455033856 | bytes 19922944 | tf_op jit(solution)/shard_map/sekd,sekh->deh/dot_general | solution.py:79
  250.7 21.4 %convert_bitcast_fusion = bf16[32,2,16,2048]{3,2,0,1:T(8,128)(2,1)S(1)} fusion(bf16[2048,2,1536,1]{2,1,0,3:T(2,128)(2,1)} %bitcast.108, bf16[32,2,16,768]{3,2,0,1:T(8,128)(2,1)} %get-tuple-element.16, bf16[32,2,16,768]{3,2,0,1:T(8,128)(2,1)S(1)} %get-tuple-element.15), kind=kOutput, calls=%fused_computation.17 | convolution fusion | flops 6450839552 | bytes 19922944 | tf_op jit(solution)/shard_map/sekh,deh->sekd/dot_general | solution.py:72
  272.2 2.5 copy.57
  274.6 5.3 %all-to-all-start.3 = ((bf16[32,2,16,2048]{3,2,1,0:T(8,128)(2,1)}), bf16[32,2,16,2048]{3,2,1,0:T(8,128)(2,1)}, u32[]{:S(2)}, u32[]{:S(2)}) async-start(bf16[32,2,16,2048]{3,2,1,0:T(8,128)(2,1)} %copy.57), calls=%async_computation.3 | async-start | bytes 8388608 | tf_op jit(solution)/shard_map/all_to_all | solution.py:54
  280.0 5.7 %fusion.5 = bf16[768,2,2048]{0,2,1:T(8,128)(2,1)S(1)} fusion(bf16[32,2,16,2048]{3,2,1,0:T(8,128)(2,1)} %copy-done.6, bf16[32,2,16,768]{3,2,0,1:T(8,128)(2,1)S(1)} %copy-done.10), kind=kOutput, calls=%fused_computation.7 | convolution fusion | flops 3224371200 | bytes 12058624 | tf_op jit(solution)/shard_map/sekh,sekd->hed/dot_general | solution.py:80
  285.6 0.4 fusion.46
  286.1 1.7 copy-done
  287.7 0.9 dynamic-slice_bitcast_fusion
  288.7 3.2 collective-permute-start.3
  291.9 0.9 dynamic-slice_bitcast_fusion.1
  292.8 33.5 %collective-permute-done.3 = bf16[768,512]{0,1:T(8,128)(2,1)} collective-permute-done((bf16[768,512]{0,1:T(8,128)(2,1)}, bf16[768,512]{0,1:T(8,128)(2,1)}, u32[]{:S(2)}, u32[]{:S(2)}) %collective-permute-start.3) | collective-permute-done | bytes 786464 | tf_op jit(solution)/shard_map/ppermute | solution.py:109
  326.4 2.4 fusion.31
  328.8 3.6 collective-permute-start.4
  332.4 2.2 fusion.34
  334.6 31.8 %collective-permute-done.4 = bf16[768,512]{0,1:T(8,128)(2,1)} collective-permute-done((bf16[768,512]{0,1:T(8,128)(2,1)}, bf16[768,512]{0,1:T(8,128)(2,1)}, u32[]{:S(2)}, u32[]{:S(2)}) %collective-permute-start.4) | collective-permute-done | bytes 786464 | tf_op jit(solution)/shard_map/ppermute | solution.py:112
  366.4 2.4 fusion.30
  368.8 3.4 collective-permute-start.5
  372.2 2.2 fusion.33
  374.5 31.6 %collective-permute-done.5 = bf16[768,512]{0,1:T(8,128)(2,1)} collective-permute-done((bf16[768,512]{0,1:T(8,128)(2,1)}, bf16[768,512]{0,1:T(8,128)(2,1)}, u32[]{:S(2)}, u32[]{:S(2)}) %collective-permute-start.5) | collective-permute-done | bytes 786464 | tf_op jit(solution)/shard_map/ppermute | solution.py:112
  406.1 1.6 fusion.40
  407.6 4.0 collective-permute-done.2
  411.6 1.3 fusion.39
  413.0 0.1 pad_maximum_fusion.3
  413.1 3.0 copy.61
  416.2 3.9 fusion.28
  420.1 8.7 %copy.60 = bf16[512,2,1536]{2,1,0:T(2,128)(2,1)} copy(bf16[512,2,1536]{0,2,1:T(8,128)(2,1)} %reduce-scatter.2.cloned.1.call-done) | data formatting | bytes 6291456
  (43 shorter events, 0.4 us)
Async XLA Ops:
  11.8 2.5 copy-start.4
  73.4 12.4 %copy-start.7 = (bf16[32,2,16,2048]{3,2,1,0:T(8,128)(2,1)}, bf16[32,2,16,2048]{3,2,1,0:T(8,128)(2,1)S(1)}, u32[]{:S(2)}) copy-start(bf16[32,2,16,2048]{3,2,1,0:T(8,128)(2,1)S(1)} %all_to_all.20) | copy-start | bytes 12582916
  85.8 2.7 copy-start.3
  88.5 11.8 %copy-start.9 = (bf16[32,2,16,768]{3,2,0,1:T(8,128)(2,1)}, bf16[32,2,16,768]{3,2,0,1:T(8,128)(2,1)S(1)}, u32[]{:S(2)}) copy-start(bf16[32,2,16,768]{3,2,0,1:T(8,128)(2,1)S(1)} %multiply_convert_fusion) | copy-start | bytes 4718596
  102.8 5.1 %copy-start.12 = (f32[160,4]{0,1:T(4,128)S(1)}, f32[160,4]{0,1:T(4,128)}, u32[]{:S(2)}) copy-start(f32[160,4]{0,1:T(4,128)} %param.9) | copy-start | bytes 7684
  102.8 57.0 %all-to-all-start.1 = ((bf16[32,2,16,2048]{3,2,1,0:T(8,128)(2,1)}), bf16[32,2,16,2048]{3,2,1,0:T(8,128)(2,1)}, u32[]{:S(2)}, u32[]{:S(2)}) async-start(bf16[32,2,16,2048]{3,2,1,0:T(8,128)(2,1)} %copy.53), calls=%async_computation.1 | async-start | bytes 8388608 | tf_op jit(solution)/shard_map/all_to_all | solution.py:54
  107.6 312.5 %reduce-scatter.2.cloned.1.call-start = ((), (), s32[]{:S(2)}) async-start(), calls=%async_computation.5 | async-start | bytes 15728640 | tf_op jit(solution)/shard_map/reduce_scatter | solution.py:84
  159.8 5.7 %copy-start.8 = (bf16[160,2048]{1,0:T(8,128)(2,1)S(1)}, bf16[160,2048]{1,0:T(8,128)(2,1)}, u32[]{:S(2)}) copy-start(bf16[160,2048]{1,0:T(8,128)(2,1)} %param.6) | copy-start | bytes 1966084
  159.8 5.8 %copy-start.11 = (bf16[160,2048]{1,0:T(8,128)(2,1)S(1)}, bf16[160,2048]{1,0:T(8,128)(2,1)}, u32[]{:S(2)}) copy-start(bf16[160,2048]{1,0:T(8,128)(2,1)} %param.7) | copy-start | bytes 1966084
  165.8 4.3 copy-start.1
  165.8 61.9 %slice-start = ((s8[6291456]{0:T(1024)(128)(4,1)}), s8[4194304]{0:T(1024)(128)(4,1)S(1)}, s32[]{:S(2)}) async-start(s8[6291456]{0:T(1024)(128)(4,1)} %bitcast.99), calls=%async_computation.6 | async-start | bytes 8388608
  166.2 61.5 %slice-start.1 = ((s8[6291456]{0:T(1024)(128)(4,1)}), s8[2097152]{0:T(1024)(128)(4,1)S(1)}, s32[]{:S(2)}) async-start(s8[6291456]{0:T(1024)(128)(4,1)} %bitcast.99), calls=%async_computation.7 | async-start | bytes 4194304
  227.7 11.2 %copy-start.6 = (bf16[32,2,16,2048]{3,2,1,0:T(8,128)(2,1)}, bf16[32,2,16,2048]{3,2,1,0:T(8,128)(2,1)S(1)}, u32[]{:S(2)}) copy-start(bf16[32,2,16,2048]{3,2,1,0:T(8,128)(2,1)S(1)} %all_to_all.21) | copy-start | bytes 12582916
  274.6 5.3 %copy-start.10 = (bf16[32,2,16,768]{3,2,0,1:T(8,128)(2,1)S(1)}, bf16[32,2,16,768]{3,2,0,1:T(8,128)(2,1)}, u32[]{:S(2)}) copy-start(bf16[32,2,16,768]{3,2,0,1:T(8,128)(2,1)} %copy-done.9) | copy-start | bytes 4718596
  274.6 141.5 %all-to-all-start.3 = ((bf16[32,2,16,2048]{3,2,1,0:T(8,128)(2,1)}), bf16[32,2,16,2048]{3,2,1,0:T(8,128)(2,1)}, u32[]{:S(2)}, u32[]{:S(2)}) async-start(bf16[32,2,16,2048]{3,2,1,0:T(8,128)(2,1)} %copy.57), calls=%async_computation.3 | async-start | bytes 8388608 | tf_op jit(solution)/shard_map/all_to_all | solution.py:54
  286.1 1.7 copy-start
  288.7 37.7 %collective-permute-start.3 = (bf16[768,512]{0,1:T(8,128)(2,1)}, bf16[768,512]{0,1:T(8,128)(2,1)}, u32[]{:S(2)}, u32[]{:S(2)}) collective-permute-start(bf16[768,512]{0,1:T(8,128)(2,1)} %dynamic-slice_bitcast_fusion), channel_id=1, source_target_pairs={{0,96},{32,0},{64,32},{96,64},{1,97},{33,1},{65,33},{97,65},{2,98}... | collective-permute-start | bytes 2359304 | tf_op jit(solution)/shard_map/ppermute | solution.py:109
  292.8 39.6 %collective-permute-start = (bf16[768,512]{0,1:T(8,128)(2,1)}, bf16[768,512]{0,1:T(8,128)(2,1)}, u32[]{:S(2)}, u32[]{:S(2)}) collective-permute-start(bf16[768,512]{0,1:T(8,128)(2,1)} %dynamic-slice_bitcast_fusion.1), channel_id=1, source_target_pairs={{0,32},{32,64},{64,96},{96,0},{1,33},{33,65},{65,97},{97,1},{2,34}... | collective-permute-start | bytes 2359304 | tf_op jit(solution)/shard_map/ppermute | solution.py:108
  328.8 37.5 %collective-permute-start.4 = (bf16[768,512]{0,1:T(8,128)(2,1)}, bf16[768,512]{0,1:T(8,128)(2,1)}, u32[]{:S(2)}, u32[]{:S(2)}) collective-permute-start(bf16[768,512]{0,1:T(8,128)(2,1)} %fusion.31), channel_id=1, source_target_pairs={{0,96},{32,0},{64,32},{96,64},{1,97},{33,1},{65,33},{97,65},{2,98}... | collective-permute-start | bytes 2359304 | tf_op jit(solution)/shard_map/ppermute | solution.py:112
  334.6 37.6 %collective-permute-start.1 = (bf16[768,512]{0,1:T(8,128)(2,1)}, bf16[768,512]{0,1:T(8,128)(2,1)}, u32[]{:S(2)}, u32[]{:S(2)}) collective-permute-start(bf16[768,512]{0,1:T(8,128)(2,1)} %fusion.34), channel_id=1, source_target_pairs={{0,32},{32,64},{64,96},{96,0},{1,33},{33,65},{65,97},{97,1},{2,34}... | collective-permute-start | bytes 2359304 | tf_op jit(solution)/shard_map/ppermute | solution.py:111
  368.8 37.3 %collective-permute-start.5 = (bf16[768,512]{0,1:T(8,128)(2,1)}, bf16[768,512]{0,1:T(8,128)(2,1)}, u32[]{:S(2)}, u32[]{:S(2)}) collective-permute-start(bf16[768,512]{0,1:T(8,128)(2,1)} %fusion.30), channel_id=1, source_target_pairs={{0,96},{32,0},{64,32},{96,64},{1,97},{33,1},{65,33},{97,65},{2,98}... | collective-permute-start | bytes 2359304 | tf_op jit(solution)/shard_map/ppermute | solution.py:112
  374.4 37.2 %collective-permute-start.2 = (bf16[768,512]{0,1:T(8,128)(2,1)}, bf16[768,512]{0,1:T(8,128)(2,1)}, u32[]{:S(2)}, u32[]{:S(2)}) collective-permute-start(bf16[768,512]{0,1:T(8,128)(2,1)} %fusion.33), channel_id=1, source_target_pairs={{0,32},{32,64},{64,96},{96,0},{1,33},{33,65},{65,97},{97,1},{2,34}... | collective-permute-start | bytes 2359304 | tf_op jit(solution)/shard_map/ppermute | solution.py:111
  413.0 3.2 copy-start.2
  413.0 3.2 copy-start.5
Sparse Core Ops, SparseCore 0:
  250.8 163.3 reduce-scatter.1

commit v6 on v2

--- a/solution.py
+++ b/solution.py
@@ -53,13 +53,31 @@
     def exchange(buffer):
         return lax.all_to_all(buffer, "expert", split_axis=0, concat_axis=0, tiled=True)
 
+    def mm(left, right, contract):
+        return lax.dot_general(
+            left, right, ((contract[0], contract[1]), ((), ())), preferred_element_type=jnp.float32
+        )
+
+    weights_in = [w_in[:, e, :] for e in range(local_experts)]
+    weights_out = [w_out[:, e, :] for e in range(local_experts)]
+
+    def rows_of(buffer, e):
+        return buffer[:, e].reshape(expert_peers * slots_per, buffer.shape[-1])
+
+    def gather_experts(parts):
+        return jnp.stack(
+            [part.reshape(expert_peers, slots_per, part.shape[-1]) for part in parts], axis=1
+        )
+
     sent_rows = exchange(to_slots(token_onehot, tokens))
-    preact = jnp.einsum("sekd,deh->sekh", sent_rows, w_in, preferred_element_type=jnp.float32)
-    activation = swiglu_forward(preact, hidden).astype(jnp.bfloat16)
-    outputs = jnp.einsum(
-        "sekh,hed->sekd", activation, w_out, preferred_element_type=jnp.float32
-    ).astype(jnp.bfloat16)
-    returned = exchange(outputs).reshape(slot_total, model_width)
+    preact, activation, outputs = [], [], []
+    for e in range(local_experts):
+        preact_e = mm(rows_of(sent_rows, e), weights_in[e], ((1,), (0,)))
+        activation_e = swiglu_forward(preact_e, hidden).astype(jnp.bfloat16)
+        outputs.append(mm(activation_e, weights_out[e], ((1,), (0,))).astype(jnp.bfloat16))
+        preact.append(preact_e)
+        activation.append(activation_e)
+    returned = exchange(gather_experts(outputs)).reshape(slot_total, model_width)
     route_rows = jnp.dot(route_onehot, returned, preferred_element_type=jnp.float32)
     student = tokens.astype(jnp.float32) + jnp.sum(
         route_rows.reshape(route_count, tok_rows, model_width) * gate_rows[:, :, None], axis=0
@@ -67,28 +85,21 @@
     residual_grad = student - target.astype(jnp.float32)
     scaled = (gate_rows[:, :, None] * residual_grad[None, :, :]).astype(jnp.bfloat16)
     sent_grads = exchange(to_slots(route_onehot, scaled.reshape(routes, model_width)))
-    act_grad = jnp.einsum("sekd,hed->sekh", sent_grads, w_out, preferred_element_type=jnp.float32)
-    pre_grad = swiglu_backward(preact, act_grad, hidden).astype(jnp.bfloat16)
-    input_grads = jnp.einsum(
-        "sekh,deh->sekd", pre_grad, w_in, preferred_element_type=jnp.float32
-    ).astype(jnp.bfloat16)
-    returned_grads = exchange(input_grads).reshape(slot_total, model_width)
+    input_grads, terms_in, terms_out = [], [], []
+    for e in range(local_experts):
+        grads_e = rows_of(sent_grads, e)
+        terms_out.append(mm(activation[e], grads_e, ((0,), (0,))).astype(jnp.bfloat16))
+        act_grad_e = mm(grads_e, weights_out[e], ((1,), (1,)))
+        pre_grad_e = swiglu_backward(preact[e], act_grad_e, hidden).astype(jnp.bfloat16)
+        input_grads.append(mm(pre_grad_e, weights_in[e], ((1,), (1,))).astype(jnp.bfloat16))
+        terms_in.append(mm(rows_of(sent_rows, e), pre_grad_e, ((0,), (0,))).astype(jnp.bfloat16))
+    returned_grads = exchange(gather_experts(input_grads)).reshape(slot_total, model_width)
     grad_tokens = (
         residual_grad + jnp.dot(token_onehot, returned_grads, preferred_element_type=jnp.float32)
     ).astype(jnp.bfloat16)
-    term_in = jnp.einsum("sekd,sekh->deh", sent_rows, pre_grad, preferred_element_type=jnp.float32)
-    term_out = jnp.einsum(
-        "sekh,sekd->hed", activation, sent_grads, preferred_element_type=jnp.float32
-    )
-    grad_in, grad_out = (
-        lax.psum_scatter(
-            term_in.astype(jnp.bfloat16), "dp", scatter_dimension=0, tiled=True
-        ).astype(jnp.float32),
-        lax.psum_scatter(
-            term_out.astype(jnp.bfloat16), "dp", scatter_dimension=2, tiled=True
-        ).astype(jnp.float32),
-    )
-    return (grad_tokens, grad_in.astype(jnp.bfloat16), grad_out.astype(jnp.bfloat16))
+    grad_out = lax.psum_scatter(jnp.stack(terms_out, axis=0), "dp", scatter_dimension=2, tiled=True)
+    grad_in = lax.psum_scatter(jnp.stack(terms_in, axis=0), "dp", scatter_dimension=1, tiled=True)
+    return (grad_tokens, jnp.transpose(grad_in, (1, 0, 2)), jnp.transpose(grad_out, (1, 0, 2)))
 
 
 def solution(mesh):

time: 431 us -> 437 us (1.014); the launches traced: 430 us -> 431 us
  blocking collectives: 171 us -> 112 us
  local copies, waits for them, and re-layouts: 22.4 us -> 59.2 us
  other arithmetic: 4.3 us -> 15.7 us
  starting transfers between devices: 5.04 us -> 16 us
    all_to_all x3 -> x2, blocking collectives: 171 us -> 112 us  [exchange(): lax.all_to_all(buffer, 'expert', split_axis=0, concat_axis=0, tiled=True)]
    slice x1 -> x5, local copies, waits for them, and re-layouts: 0.27 us -> 42.3 us  [the longest x1 25.2 us: per_device(): weights_in = [w_in[:, e, :] for e in range(local_experts)]]
    all_to_all x1 -> x2, waiting for transfers between devices: 51.9 us -> 65.3 us  [exchange(): lax.all_to_all(buffer, 'expert', split_axis=0, concat_axis=0, tiled=True)]
    another operation x2 -> x6, other arithmetic: 1.52 us -> 12.9 us  [the longest x1 5.54 us: per_device(): jnp.stack(terms_in, axis=0)]
    all_to_all x1 -> x2, starting transfers between devices: 4.78 us -> 16 us  [exchange(): lax.all_to_all(buffer, 'expert', split_axis=0, concat_axis=0, tiled=True)]
    reduce_scatter x2, waiting for transfers between devices: 85 us -> 74.5 us  [the longest x1 74.5 us: per_device(): lax.psum_scatter(jnp.stack(terms_in, axis=0), 'dp', scatter_dimension=1,...]
    dot_general x6 -> x12, matrix products: 61.9 us -> 57.3 us  [mm(): lax.dot_general(left, right, ((contract[0], contract[1]), ((), ())), pref...]
    unnamed x24 -> x46, local copies, waits for them, and re-layouts: 17.4 us -> 15.2 us
  transfers between devices with their start and end apart: 3 -> 4, of which waited for: 2 -> 3; matrix products, arithmetic and copies ran while one was open for 9% -> 21% of each run, Pallas kernels for 0% -> 0%
where the time goes in v6:
time: 437 us; the launch traced here: 431 us
  waiting for transfers between devices  140 us (32%)
  blocking collectives  112 us (26%)
  matrix products  73.4 us (17%)
  local copies, waits for them, and re-layouts  59.2 us (14%)
  starting transfers between devices  16 us (4%)
  other arithmetic  15.7 us (4%)
  between operations  14.7 us (3%)
    all_to_all x2, blocking collectives, exchange(): lax.all_to_all(buffer, 'expert', split_axis=0, concat_axis=0, tiled=True)  112 us
    reduce_scatter x1, waiting for transfers between devices, per_device(): lax.psum_scatter(jnp.stack(terms_in, axis=0), 'dp', scatter_dimension=1,...  74.5 us
    all_to_all x2, waiting for transfers between devices, exchange(): lax.all_to_all(buffer, 'expert', split_axis=0, concat_axis=0, tiled=True)  65.3 us
    dot_general x12, matrix products, mm(): lax.dot_general(left, right, ((contract[0], contract[1]), ((), ())), pref...  57.3 us
    slice x1, local copies, waits for them, and re-layouts, per_device(): weights_in = [w_in[:, e, :] for e in range(local_experts)]  25.2 us
    all_to_all x2, starting transfers between devices, exchange(): lax.all_to_all(buffer, 'expert', split_axis=0, concat_axis=0, tiled=True)  16 us
    unnamed x46, local copies, waits for them, and re-layouts  15.2 us
    slice x1, local copies, waits for them, and re-layouts, per_device(): weights_out = [w_out[:, e, :] for e in range(local_experts)]  13.8 us
  transfers between devices with their start and end apart: 4, of which 3 were waited for; matrix products, arithmetic and copies ran while one was open for 21% of the time, Pallas kernels for 0%

profile of v6, /device:TPU:1, one launch (start us, length us, event | category | flops | bytes accessed | tf_op | source)
XLA Modules:
  0.0 431.0 jit_solution(10795328757135238355)
XLA Ops:
  7.2 0.8 eq.67
  7.9 0.8 eq.71
  8.7 1.5 reduce-window.6
  10.2 0.3 slice_reduce_fusion
  10.5 0.1 fusion.19
  10.7 0.7 multiply_add_fusion.1
  11.4 0.4 fusion.13
  11.8 4.3 %convolution_convert_fusion.3 = bf16[1024,2048]{1,0:T(8,128)(2,1)} fusion(bf16[160,1024]{1,0:T(8,128)(2,1)S(1)} %fusion.13, bf16[160,2048]{1,0:T(8,128)(2,1)} %param.6), kind=kOutput, calls=%fused_computation.14 | convolution fusion | flops 673185792 | bytes 5177344 | tf_op jit(solution)/shard_map/dot_general | solution.py:48
  16.1 8.6 %all-to-all-start = ((bf16[32,2,16,2048]{3,2,1,0:T(8,128)(2,1)}), bf16[32,2,16,2048]{3,2,1,0:T(8,128)(2,1)}, u32[]{:S(2)}, u32[]{:S(2)}) async-start(bf16[32,2,16,2048]{3,2,1,0:T(8,128)(2,1)} %bitcast.96), calls=%async_computation | async-start | bytes 8388608 | tf_op jit(solution)/shard_map/all_to_all | solution.py:54
  24.8 13.8 %fusion.26 = (bf16[768,1,2048]{2,1,0:T(2,128)(2,1)}, bf16[768,1,2048]{2,1,0:T(2,128)(2,1)}) fusion(bf16[768,2,2048]{2,1,0:T(2,128)(2,1)} %param.11), kind=kLoop, calls=%fused_computation.67 | loop fusion | bytes 12582912 | tf_op jit(solution)/shard_map/slice | solution.py:62
  38.5 25.2 %fusion.25 = (bf16[2048,1,1536]{2,1,0:T(2,128)(2,1)}, bf16[2048,1,1536]{2,1,0:T(2,128)(2,1)}) fusion(bf16[2048,2,1536]{2,1,0:T(2,128)(2,1)} %param.10), kind=kLoop, calls=%fused_computation.66 | loop fusion | bytes 25165824 | tf_op jit(solution)/shard_map/slice | solution.py:61
  63.8 13.2 %all-to-all-done = bf16[32,2,16,2048]{3,2,1,0:T(8,128)(2,1)} async-done(((bf16[32,2,16,2048]{3,2,1,0:T(8,128)(2,1)}), bf16[32,2,16,2048]{3,2,1,0:T(8,128)(2,1)}, u32[]{:S(2)}, u32[]{:S(2)}) %all-to-all-start) | async-done | bytes 4194336 | tf_op jit(solution)/shard_map/all_to_all | solution.py:54
  77.0 2.7 fusion.28
  79.7 1.3 copy-done.4
  81.0 7.1 %fusion.9 = f32[512,1536]{1,0:T(8,128)S(1)} fusion(bf16[512,2048]{1,0:T(8,128)(2,1)S(1)} %bitcast.106, bf16[2048,1,1536]{2,1,0:T(2,128)(2,1)} %get-tuple-element.15), kind=kOutput, calls=%fused_computation.32 | convolution fusion | flops 3221225472 | bytes 11534336 | tf_op jit(solution)/shard_map/dot_general | solution.py:57
  88.2 1.6 copy-done
  89.8 0.5 multiply_convert_fusion.5
  90.3 3.4 fusion.10
  93.8 0.5 multiply_convert_fusion.4
  94.3 2.2 convolution_convert_fusion.9
  96.6 0.5 slice-done.5
  97.1 0.7 slice-done.6
  97.8 2.2 convolution_convert_fusion.8
  100.0 2.3 pad_maximum_fusion.2
  102.3 7.3 %all-to-all-start.1 = ((bf16[32,2,16,2048]{3,2,1,0:T(8,128)(2,1)}), bf16[32,2,16,2048]{3,2,1,0:T(8,128)(2,1)}, u32[]{:S(2)}, u32[]{:S(2)}) async-start(bf16[32,2,16,2048]{3,2,1,0:T(8,128)(2,1)} %pad_maximum_fusion.2), calls=%async_computation.1 | async-start | bytes 8388608 | tf_op jit(solution)/shard_map/all_to_all | solution.py:54
  109.8 52.1 %all-to-all-done.1 = bf16[32,2,16,2048]{3,2,1,0:T(8,128)(2,1)} async-done(((bf16[32,2,16,2048]{3,2,1,0:T(8,128)(2,1)}), bf16[32,2,16,2048]{3,2,1,0:T(8,128)(2,1)}, u32[]{:S(2)}, u32[]{:S(2)}) %all-to-all-start.1) | async-done | bytes 4194336 | tf_op jit(solution)/shard_map/all_to_all | solution.py:54
  161.8 6.1 %multiply_reduce_fusion = f32[160,2048]{1,0:T(8,128)S(1)} fusion(bf16[1024,2048,1]{1,0,2:T(8,128)(2,1)} %bitcast.15, f32[4,160]{1,0:T(4,128)S(1)} %bitcast.123, s32[4,160]{1,0:T(4,128)S(1)} %multiply_add_fusion.1), kind=kOutput, calls=%fused_computation.10 | convolution fusion | flops 2687303680 | bytes 5510144 | tf_op jit(solution)/shard_map/dot_general | solution.py:81
  167.9 0.2 convert_subtract_fusion
  168.2 0.3 fusion.2
  168.5 4.0 convolution_convert_fusion.2
  172.5 57.5 %all_to_all.20 = bf16[32,2,16,2048]{3,2,1,0:T(8,128)(2,1)S(1)} all-to-all(bf16[32,2,16,2048]{3,2,1,0:T(8,128)(2,1)S(1)} %bitcast.104), channel_id=1, replica_groups=mesh['dp'=4,'expert'=32] {'expert'}, dimensions={0} | all-to-all | bytes 8388608 | tf_op jit(solution)/shard_map/all_to_all | solution.py:54
  230.0 0.3 fusion.27
  230.3 1.9 fusion.4
  232.3 1.9 fusion.3
  234.2 3.2 pad_maximum_fusion.1
  237.4 7.3 %multiply_convert_fusion.1 = (bf16[512,768]{1,0:T(8,128)(2,1)S(1)}, bf16[512,768]{1,0:T(8,128)(2,1)S(1)}) fusion(f32[512,1536]{1,0:T(8,128)} %copy-done.2, bf16[512,2048]{1,0:T(8,128)(2,1)} %bitcast.113, bf16[768,1,2048]{2,1,0:T(2,128)(2,1)} %get-tuple-element.18), kind=kOutput, calls=%fused_computation.37 | convolution fusion | flops 1615724544 | bytes 9961472 | tf_op jit(solution)/shard_map/dot_general | solution.py:57
  244.8 4.0 fusion.1
  248.9 6.0 %multiply_convert_fusion.3 = (bf16[512,768]{1,0:T(8,128)(2,1)S(1)}, bf16[512,768]{1,0:T(8,128)(2,1)S(1)}) fusion(f32[512,1536]{1,0:T(8,128)S(1)} %copy-done.1, bf16[512,2048]{1,0:T(8,128)(2,1)S(1)} %bitcast.111, bf16[768,1,2048]{2,1,0:T(2,128)(2,1)} %get-tuple-element.17), kind=kOutput, calls=%fused_computation.39 | convolution fusion | flops 1615724544 | bytes 9961472 | tf_op jit(solution)/shard_map/dot_general | solution.py:57
  254.9 3.9 fusion
  258.8 5.5 %pad_maximum_fusion = bf16[2,2048,1536]{2,1,0:T(8,128)(2,1)} fusion(bf16[1,2048,1536]{2,1,0:T(8,128)(2,1)S(1)} %fusion.1, bf16[1,2048,1536]{2,1,0:T(8,128)(2,1)S(1)} %fusion), kind=kLoop, calls=%fused_computation | loop fusion | flops 6291456 | bytes 25165824 | tf_op jit(solution)/shard_map/stack | solution.py:101
  264.4 8.7 %convolution_convert_fusion.7 = bf16[512,2048]{1,0:T(8,128)(2,1)S(1)} fusion(bf16[2048,1,1536]{2,1,0:T(2,128)(2,1)} %get-tuple-element.15, bf16[512,768]{1,0:T(8,128)(2,1)} %copy-done.14, bf16[512,768]{1,0:T(8,128)(2,1)} %copy-done.13), kind=kOutput, calls=%fused_computation.20 | convolution fusion | flops 3225419776 | bytes 9961472 | tf_op jit(solution)/shard_map/dot_general | solution.py:57
  273.1 8.6 %convolution_convert_fusion.6 = bf16[512,2048]{1,0:T(8,128)(2,1)S(1)} fusion(bf16[2048,1,1536]{2,1,0:T(2,128)(2,1)} %get-tuple-element.16, bf16[512,768]{1,0:T(8,128)(2,1)S(1)} %get-tuple-element.22, bf16[512,768]{1,0:T(8,128)(2,1)S(1)} %get-tuple-element.21), kind=kOutput, calls=%fused_computation.19 | convolution fusion | flops 3225419776 | bytes 9961472 | tf_op jit(solution)/shard_map/dot_general | solution.py:57
  281.7 0.4 pad_maximum_fusion.3
  282.1 54.6 %all_to_all.21 = bf16[32,2,16,2048]{3,2,1,0:T(8,128)(2,1)S(1)} all-to-all(bf16[32,2,16,2048]{3,2,1,0:T(8,128)(2,1)S(1)} %pad_maximum_fusion.3), channel_id=1, replica_groups=mesh['dp'=4,'expert'=32] {'expert'}, dimensions={0} | all-to-all | bytes 8388608 | tf_op jit(solution)/shard_map/all_to_all | solution.py:54
  336.7 1.8 fusion.8
  338.5 4.2 copy.43
  342.6 74.5 %reduce-scatter.3.cloned.1.call-done = bf16[2,512,1536]{2,1,0:T(8,128)(2,1)} async-done(((bf16[2,2048,1536]{2,1,0:T(8,128)(2,1)}), bf16[2,512,1536]{2,1,0:T(8,128)(2,1)}) %reduce-scatter.3.cloned.1.call-update) | async-done | bytes 3145744 | tf_op jit(solution)/shard_map/reduce_scatter | solution.py:101
  417.1 6.8 %copy.42 = bf16[512,2,1536]{2,1,0:T(2,128)(2,1)} copy(bf16[512,2,1536]{2,0,1:T(8,128)(2,1)} %bitcast.105) | data formatting | bytes 6291456
  (53 shorter events, 0.5 us)
Async XLA Ops:
  16.1 60.9 %all-to-all-start = ((bf16[32,2,16,2048]{3,2,1,0:T(8,128)(2,1)}), bf16[32,2,16,2048]{3,2,1,0:T(8,128)(2,1)}, u32[]{:S(2)}, u32[]{:S(2)}) async-start(bf16[32,2,16,2048]{3,2,1,0:T(8,128)(2,1)} %bitcast.96), calls=%async_computation | async-start | bytes 8388608 | tf_op jit(solution)/shard_map/all_to_all | solution.py:54
  77.0 13.3 %slice-start = ((s8[12582912]{0:T(1024)(128)(4,1)}), s8[4194304]{0:T(1024)(128)(4,1)S(1)}, s32[]{:S(2)}) async-start(s8[12582912]{0:T(1024)(128)(4,1)} %bitcast.98), calls=%async_computation.8 | async-start | bytes 8388608
  79.7 1.3 copy-start.4
  79.7 10.6 %copy-start.6 = (bf16[32,1,16,2048]{3,2,1,0:T(8,128)(2,1)}, bf16[32,1,16,2048]{3,2,1,0:T(8,128)(2,1)S(1)}, u32[]{:S(2)}) copy-start(bf16[32,1,16,2048]{3,2,1,0:T(8,128)(2,1)S(1)} %get-tuple-element.26) | copy-start | bytes 6291460
  81.0 9.3 %slice-start.1 = ((s8[12582912]{0:T(1024)(128)(4,1)}), s8[4194304]{0:T(1024)(128)(4,1)S(1)}, s32[]{:S(2)}) async-start(s8[12582912]{0:T(1024)(128)(4,1)} %bitcast.98), calls=%async_computation.9 | async-start | bytes 8388608
  81.0 9.3 %slice-start.2 = ((s8[12582912]{0:T(1024)(128)(4,1)}), s8[4194304]{0:T(1024)(128)(4,1)S(1)}, s32[]{:S(2)}) async-start(s8[12582912]{0:T(1024)(128)(4,1)} %bitcast.98), calls=%async_computation.10 | async-start | bytes 8388608
  88.1 1.6 copy-start
  89.8 4.5 %slice-start.3 = ((s8[6291456]{0:T(1024)(128)(4,1)}), s8[4194304]{0:T(1024)(128)(4,1)S(1)}, s32[]{:S(2)}) async-start(s8[6291456]{0:T(1024)(128)(4,1)} %bitcast.100), calls=%async_computation.11 | async-start | bytes 8388608
  90.3 3.9 slice-start.4
  93.8 2.8 copy-start.2
  93.8 3.3 slice-start.5
  94.3 3.5 slice-start.6
  102.3 7.4 %copy-start.12 = (f32[160,4]{0,1:T(4,128)S(1)}, f32[160,4]{0,1:T(4,128)}, u32[]{:S(2)}) copy-start(f32[160,4]{0,1:T(4,128)} %param.9) | copy-start | bytes 7684
  102.3 59.5 %all-to-all-start.1 = ((bf16[32,2,16,2048]{3,2,1,0:T(8,128)(2,1)}), bf16[32,2,16,2048]{3,2,1,0:T(8,128)(2,1)}, u32[]{:S(2)}, u32[]{:S(2)}) async-start(bf16[32,2,16,2048]{3,2,1,0:T(8,128)(2,1)} %pad_maximum_fusion.2), calls=%async_computation.1 | async-start | bytes 8388608 | tf_op jit(solution)/shard_map/all_to_all | solution.py:54
  109.6 228.9 %reduce-scatter.5.cloned.1.call-start = ((), (), s32[]{:S(2)}) async-start(), calls=%async_computation.7 | async-start | bytes 7864320 | tf_op jit(solution)/shard_map/reduce_scatter | solution.py:100
  161.8 6.1 %copy-start.3 = (bf16[160,2048]{1,0:T(8,128)(2,1)S(1)}, bf16[160,2048]{1,0:T(8,128)(2,1)}, u32[]{:S(2)}) copy-start(bf16[160,2048]{1,0:T(8,128)(2,1)} %param.6) | copy-start | bytes 1966084
  161.8 6.1 %copy-start.11 = (bf16[160,2048]{1,0:T(8,128)(2,1)S(1)}, bf16[160,2048]{1,0:T(8,128)(2,1)}, u32[]{:S(2)}) copy-start(bf16[160,2048]{1,0:T(8,128)(2,1)} %param.7) | copy-start | bytes 1966084
  230.3 1.9 copy-start.10
  230.3 2.0 copy-start.8
  237.4 179.7 %reduce-scatter.3.cloned.1.call-start = ((), (), s32[]{:S(2)}) async-start(), calls=%async_computation.6 | async-start | bytes 15728640 | tf_op jit(solution)/shard_map/reduce_scatter | solution.py:101
  237.4 7.3 %copy-start.7 = (bf16[32,1,16,2048]{3,2,1,0:T(8,128)(2,1)S(1)}, bf16[32,1,16,2048]{3,2,1,0:T(8,128)(2,1)}, u32[]{:S(2)}) copy-start(bf16[32,1,16,2048]{3,2,1,0:T(8,128)(2,1)} %copy-done.6) | copy-start | bytes 6291460
  244.8 4.1 copy-start.1
  244.8 4.1 copy-start.9
  248.9 6.1 %copy-start.5 = (bf16[32,1,16,2048]{3,2,1,0:T(8,128)(2,1)S(1)}, bf16[32,1,16,2048]{3,2,1,0:T(8,128)(2,1)}, u32[]{:S(2)}) copy-start(bf16[32,1,16,2048]{3,2,1,0:T(8,128)(2,1)} %copy-done.4) | copy-start | bytes 6291460
  254.9 3.9 copy-start.13
  254.9 3.9 copy-start.14
Sparse Core Ops, SparseCore 0:
  237.5 62.7 reduce-scatter.4
  302.8 114.2 reduce-scatter.2
